TPU v7x, 256 devices: a whole 4x4x8 slice. The times are simulated.
256 devices in a mesh: expert: 8 (over z_lo, core), tensor: 32 (over z_hi, x, y).
Axes of the slice: x: 4, y: 4, z: 8 (z_hi: 2, z_lo: 4; z = z_hi * 4 + z_lo), core: 2. Of those that a mesh axis runs over, the one named last changes fastest.
Arguments:
- tokens: bfloat16 [2048, 6144], P('expert', 'tensor'), may hold values from -6 to 6
- router_weight: bfloat16 [6144, 8], replicated, may hold values from -0.078125 to 0.078125
- expert_ids: int32 [2048, 2], P('expert'), may hold values from 0 to 7, all different within a row
- w_gate: bfloat16 [8, 6144, 8192], P('expert', None, 'tensor'), may hold values from -0.078125 to 0.078125
- w_up: bfloat16 [8, 6144, 8192], P('expert', None, 'tensor'), may hold values from -0.078125 to 0.078125
- w_down: bfloat16 [8, 8192, 6144], P('expert', 'tensor'), may hold values from -0.125 to 0.125
Outputs:
- moe_out: bfloat16 [2048, 6144], P('expert', 'tensor')
Inputs may be any that keep to these rules, and one draw needn't show every extreme that they name: `expert_ids`: each row names 2 different experts, and every expert is named by some row.
All inputs are finite; a program needn't handle non-finite values.
Results may differ from a plain program's by a relative error of at most 0.03.
Values may be sent and summed in bfloat16 or wider, within the bound.
No kernel may reach another device: no remote copies, remote signals or barrier semaphores. Data moves between devices by JAX's collectives and lax.ppermute only.
A program may use at most 64 MiB of HBM per device.

v0:
```python
import jax
import jax.numpy as jnp
from jax import lax
from jax.sharding import PartitionSpec as P


def body(tokens, router_weight, expert_ids, w_gate, w_up, w_down):
    tok_rows, part_width = tokens.shape
    top_count = expert_ids.shape[1]
    n_experts = lax.axis_size("expert")
    capacity = 5 * tok_rows * top_count // (4 * n_experts)
    slots_all = n_experts * capacity
    gate_local = w_gate[0]
    up_local = w_up[0]
    down_local = w_down[0]
    rows_count = n_experts * capacity
    flat_ids = expert_ids.reshape(-1)
    picks = tok_rows * top_count
    expert_hot = (flat_ids[:, None] == jnp.arange(n_experts, dtype=jnp.int32)[None, :]).astype(
        jnp.float32
    )
    lower = (jnp.arange(picks)[:, None] > jnp.arange(picks)[None, :]).astype(jnp.float32)
    before = jnp.dot(lower, expert_hot, precision=lax.Precision.HIGHEST)
    slot_pos = jnp.sum(before * expert_hot, axis=1).astype(jnp.int32)
    kept = slot_pos < capacity
    target = flat_ids * capacity + slot_pos
    placed = (target[:, None] == jnp.arange(slots_all, dtype=jnp.int32)[None, :]) & kept[:, None]
    placed = placed.reshape(tok_rows, top_count, slots_all).astype(jnp.float32)
    dispatch = jnp.sum(placed, axis=1).astype(jnp.bfloat16)
    contract_first = (((0,), (0,)), ((), ()))
    full_rows = lax.all_gather(tokens, "tensor", axis=1, tiled=True)
    logits = jnp.dot(full_rows, router_weight, preferred_element_type=jnp.float32)
    buckets = lax.dot_general(
        dispatch, full_rows, contract_first, preferred_element_type=jnp.float32
    ).astype(jnp.bfloat16)
    arrived = lax.all_to_all(
        buckets.reshape(n_experts, capacity, -1), "expert", split_axis=0, concat_axis=0, tiled=True
    )
    bucket_rows = arrived.reshape(rows_count, -1)
    gate = jnp.dot(bucket_rows, gate_local, preferred_element_type=jnp.float32)
    upper = jnp.dot(bucket_rows, up_local, preferred_element_type=jnp.float32)
    hidden = (jax.nn.silu(gate) * upper).astype(jnp.bfloat16)
    contract_hidden = (((0,), (1,)), ((), ()))
    summed = lax.psum_scatter(
        lax.dot_general(
            down_local, hidden, contract_hidden, preferred_element_type=jnp.float32
        ).astype(jnp.bfloat16),
        "tensor",
        scatter_dimension=0,
        tiled=True,
    )
    returned = lax.all_to_all(summed, "expert", split_axis=1, concat_axis=1, tiled=True)
    choose_hot = (
        expert_ids[:, :, None] == jnp.arange(n_experts, dtype=jnp.int32)[None, None, :]
    ).astype(jnp.float32)
    chosen = jnp.sum(choose_hot * logits[:, None, :], axis=2)
    weight = jax.nn.sigmoid(chosen - jnp.flip(chosen, axis=1)).astype(jnp.bfloat16)
    combine = jnp.sum(placed * weight.astype(jnp.float32)[:, :, None], axis=1).astype(jnp.bfloat16)
    mixed = lax.dot_general(
        combine, returned, (((1,), (1,)), ((), ())), preferred_element_type=jnp.float32
    )
    return mixed.astype(jnp.bfloat16)


def solution(mesh):
    in_specs = (
        P("expert", "tensor"),
        P(),
        P("expert", None),
        P("expert", None, "tensor"),
        P("expert", None, "tensor"),
        P("expert", "tensor", None),
    )
    out_specs = P("expert", "tensor")
    return jax.shard_map(body, mesh=mesh, in_specs=in_specs, out_specs=out_specs, check_vma=False)
```

profile of v0, /device:TPU:1, one launch (start us, length us, event | category | flops | bytes accessed | tf_op | source)
XLA Modules:
  0.0 633.0 jit_solution(9283036379071454045)
XLA Ops:
  6.5 0.7 all-gather.2.cloned.1.call-update
  7.3 0.0 reduce-scatter.4.cloned.1.call-start
  7.3 1.0 copy.26
  8.3 0.1 eq.42
  8.4 0.3 fusion.13
  8.7 0.1 convert_element_type.47
  8.9 0.1 copy.27
  8.9 0.7 multiply_add_fusion
  9.6 101.0 %all-gather.2.cloned.1.call-done = bf16[256,6144]{0,1:T(8,128)(2,1)} async-done(((bf16[256,192]{0,1:T(8,128)(2,1)}), bf16[256,6144]{0,1:T(8,128)(2,1)}) %all-gather.2.cloned.1.call-update) | async-done | bytes 3145744 | tf_op jit(solution)/shard_map/all_gather | solution.py:31
  110.6 2.4 fusion.22
  113.1 0.1 rev.4
  113.2 0.4 select_reduce_fusion
  113.6 4.2 convolution_convert_fusion.1
  117.8 0.0 copy-start.3
  117.8 179.8 %all_to_all.17 = bf16[8,80,6144]{2,1,0:T(8,128)(2,1)S(1)} all-to-all(bf16[8,80,6144]{2,1,0:T(8,128)(2,1)S(1)} %bitcast.30), channel_id=1, replica_groups=mesh['expert'=8,'tensor'=32] {'expert'}, dimensions={0} | all-to-all | bytes 15728640 | tf_op jit(solution)/shard_map/all_to_all | solution.py:36
  297.6 3.2 copy-done.1
  300.7 3.0 fusion.4
  303.8 16.6 %fusion = bf16[6144,640]{0,1:T(8,128)(2,1)} fusion(bf16[1,256,6144]{2,1,0:T(8,128)(2,1)S(1)} %copy-done, bf16[640,6144]{1,0:T(8,128)(2,1)} %bitcast.32, bf16[1,6144,256]{2,1,0:T(8,128)(2,1)} %param.10, f32[640,256]{1,0:T(8,128)} %fusion.4), kind=kOutput, calls=%fused_computation.2 | convolution fusion | flops 4031447040 | bytes 22675456 | tf_op jit(solution)/shard_map/dot_general | solution.py:45
  320.4 10.6 %copy.29 = bf16[6144,640]{1,0:T(8,128)(2,1)} copy(bf16[6144,640]{0,1:T(8,128)(2,1)} %fusion) | data formatting | bytes 15728640
  331.0 0.0 reduce-scatter.4.cloned.1.call-update
  331.0 274.8 %reduce-scatter.4.cloned.1.call-done = bf16[192,640]{1,0:T(8,128)(2,1)} async-done(((bf16[6144,640]{1,0:T(8,128)(2,1)}), bf16[192,640]{1,0:T(8,128)(2,1)}) %reduce-scatter.4.cloned.1.call-update) | async-done | bytes 245776
  605.8 1.8 copy.30
  607.7 17.5 %all_to_all.18 = bf16[192,8,80]{0,2,1:T(8,128)(2,1)S(1)} all-to-all(bf16[192,8,80]{0,2,1:T(8,128)(2,1)} %bitcast.34), channel_id=1, replica_groups=mesh['expert'=8,'tensor'=32] {'expert'}, dimensions={1} | all-to-all | bytes 491520 | tf_op jit(solution)/shard_map/all_to_all | solution.py:52
  625.2 1.0 convolution_convert_fusion.2
  (11 shorter events, 0.1 us)
Async XLA Ops:
  6.5 297.2 %copy-start = (bf16[1,256,6144]{2,1,0:T(8,128)(2,1)S(1)}, bf16[1,256,6144]{2,1,0:T(8,128)(2,1)}, u32[]{:S(2)}) copy-start(bf16[1,256,6144]{2,1,0:T(8,128)(2,1)} %param.11) | copy-start | bytes 9437188
  6.5 106.5 %copy-start.2 = (s32[256,2]{0,1:T(2,128)S(1)}, s32[256,2]{0,1:T(2,128)}, u32[]{:S(2)}) copy-start(s32[256,2]{0,1:T(2,128)} %param.8) | copy-start | bytes 6148
  6.5 104.1 %all-gather.2.cloned.1.call-start = ((), (), s32[]{:S(2)}) async-start(), calls=%async_computation.3 | async-start | bytes 3244032 | tf_op jit(solution)/shard_map/all_gather | solution.py:31
  7.3 598.6 %reduce-scatter.4.cloned.1.call-start = ((), (), s32[]{:S(2)}) async-start(), calls=%async_computation.4 | async-start | bytes 8110080
  117.8 183.0 %copy-start.3 = (bf16[1,6144,256]{2,1,0:T(8,128)(2,1)S(1)}, bf16[1,6144,256]{2,1,0:T(8,128)(2,1)}, u32[]{:S(2)}) copy-start(bf16[1,6144,256]{2,1,0:T(8,128)(2,1)} %param.9) | copy-start | bytes 9437188
  297.6 3.2 copy-start.1
Sparse Core Ops, SparseCore 0:
  10.7 99.8 all-gather.1
  331.1 274.6 reduce-scatter.3
where the time goes:
time: 633 us
  waiting for transfers between devices  377 us (60%)
  blocking collectives  197 us (31%)
  matrix products  27.4 us (4%)
  local copies, waits for them, and re-layouts  17 us (3%)
  between operations  13.5 us (2%)
    unnamed x3, waiting for transfers between devices  276 us
    all_to_all x1, blocking collectives, body(): lax.all_to_all(buckets.reshape(n_experts, capacity, -1), 'expert', split_...  180 us
    all_gather x1, waiting for transfers between devices, body(): full_rows = lax.all_gather(tokens, 'tensor', axis=1, tiled=True)  101 us
    all_to_all x1, blocking collectives, body(): lax.all_to_all(summed, 'expert', split_axis=1, concat_axis=1, tiled=True)  17.5 us
    dot_general x1, matrix products, body(): lax.dot_general(down_local, hidden, contract_hidden, preferred_element_ty...  16.6 us
    unnamed x11, local copies, waits for them, and re-layouts  16.6 us
  transfers between devices with their start and end apart: 2, of which 2 were waited for; matrix products, arithmetic and copies ran while one was open for 0% of the time, Pallas kernels for 0%

commit v1 on v0

v1 whole, which is shorter than its diff:
```python
import jax
import jax.numpy as jnp
from jax import lax
from jax.sharding import Mesh
from jax.sharding import PartitionSpec as P

EXPERT = "expert"
ZH, GX, GY = "zh", "x", "y"
TENSOR = (ZH, GX, GY)


def body(tokens, router_weight, expert_ids, w_gate, w_up, w_down):
    tok_rows, part_width = tokens.shape
    top_count = expert_ids.shape[1]
    n_experts = lax.axis_size(EXPERT)
    n_hi = lax.axis_size(ZH)
    n_plane = lax.axis_size(GX) * lax.axis_size(GY)
    capacity = 5 * tok_rows * top_count // (4 * n_experts)
    slots_all = n_experts * capacity
    d_model = router_weight.shape[0]
    my_expert = lax.axis_index(EXPERT)

    flat_ids = expert_ids.reshape(-1)
    picks = tok_rows * top_count
    expert_hot = (flat_ids[:, None] == jnp.arange(n_experts, dtype=jnp.int32)[None, :]).astype(jnp.float32)
    lower = (jnp.arange(picks)[:, None] > jnp.arange(picks)[None, :]).astype(jnp.float32)
    before = jnp.dot(lower, expert_hot, precision=lax.Precision.HIGHEST)
    slot_pos = jnp.sum(before * expert_hot, axis=1).astype(jnp.int32)
    kept = slot_pos < capacity
    target = flat_ids * capacity + slot_pos
    placed = (target[:, None] == jnp.arange(slots_all, dtype=jnp.int32)[None, :]) & kept[:, None]
    placed = placed.reshape(tok_rows, top_count, slots_all).astype(jnp.float32)
    dispatch = jnp.sum(placed, axis=1).astype(jnp.bfloat16)
    other_id = jnp.flip(expert_ids, axis=1).astype(jnp.float32)
    other_of_slot = jnp.sum(placed * other_id[:, :, None], axis=(0, 1))

    bucket_t = lax.dot_general(
        tokens, dispatch, (((0,), (0,)), ((), ())), preferred_element_type=jnp.float32
    ).astype(jnp.bfloat16)
    meta = jnp.broadcast_to(other_of_slot.astype(jnp.bfloat16)[None, :], (8, slots_all))
    payload = jnp.concatenate([bucket_t, meta], axis=0)
    arrived = lax.all_to_all(payload, EXPERT, split_axis=1, concat_axis=1, tiled=True)
    rows_t = arrived[:part_width]
    other_here = arrived[part_width].astype(jnp.int32)

    rows_t = lax.all_gather(rows_t, ZH, axis=0, tiled=True)
    rows_t = lax.all_gather(rows_t, (GX, GY), axis=0, tiled=True)

    def plane_major(w):
        tail = w.shape[1:]
        w = w.reshape((n_hi, n_plane, part_width) + tail)
        return jnp.swapaxes(w, 0, 1).reshape((d_model,) + tail)

    contract_first = (((0,), (0,)), ((), ()))
    logits = lax.dot_general(rows_t, plane_major(router_weight), contract_first, preferred_element_type=jnp.float32)
    expert_col = jnp.arange(n_experts, dtype=jnp.int32)[None, :]
    own_logit = jnp.sum(jnp.where(expert_col == my_expert, logits, 0.0), axis=1)
    other_logit = jnp.sum(jnp.where(expert_col == other_here[:, None], logits, 0.0), axis=1)
    weight = jax.nn.sigmoid(own_logit - other_logit).astype(jnp.bfloat16).astype(jnp.float32)

    gate = lax.dot_general(rows_t, plane_major(w_gate[0]), contract_first, preferred_element_type=jnp.float32)
    upper = lax.dot_general(rows_t, plane_major(w_up[0]), contract_first, preferred_element_type=jnp.float32)
    hidden = (jax.nn.silu(gate) * upper * weight[:, None]).astype(jnp.bfloat16)

    down = w_down[0]
    partial = lax.dot_general(down, hidden, (((0,), (1,)), ((), ())), preferred_element_type=jnp.float32)
    partial = plane_major(partial.astype(jnp.bfloat16))
    summed = lax.psum_scatter(partial, (GX, GY), scatter_dimension=0, tiled=True)
    summed = lax.psum_scatter(summed, ZH, scatter_dimension=0, tiled=True)
    returned = lax.all_to_all(summed, EXPERT, split_axis=1, concat_axis=1, tiled=True)

    combine = dispatch
    mixed = lax.dot_general(combine, returned, (((1,), (1,)), ((), ())), preferred_element_type=jnp.float32)
    return mixed.astype(jnp.bfloat16)


def solution(mesh):
    n_expert, n_tensor = mesh.devices.shape
    fine = Mesh(mesh.devices.reshape(n_expert, 2, 4, n_tensor // 8), (EXPERT, ZH, GX, GY))
    in_specs = (
        P(EXPERT, TENSOR),
        P(),
        P(EXPERT, None),
        P(EXPERT, None, TENSOR),
        P(EXPERT, None, TENSOR),
        P(EXPERT, TENSOR, None),
    )
    out_specs = P(EXPERT, TENSOR)
    return jax.shard_map(body, mesh=fine, in_specs=in_specs, out_specs=out_specs, check_vma=False)
```

time: 633 us -> 315 us (0.50)
  waiting for transfers between devices: 377 us -> 182 us
  blocking collectives: 197 us -> 50.8 us
  local copies, waits for them, and re-layouts: 17 us -> 37.6 us
    unnamed x3, waiting for transfers between devices: 276 us -> 0.05 us
    all_to_all x2, blocking collectives: 197 us -> 32.4 us  [the longest x1 17.9 us: body(): lax.all_to_all(payload, EXPERT, split_axis=1, concat_axis=1, tiled=True)]
    reduce_scatter x0 -> x2, waiting for transfers between devices: none -> 120 us  [the longest x1 88.5 us: body(): lax.psum_scatter(partial, (GX, GY), scatter_dimension=0, tiled=True)]
    all_gather x1, waiting for transfers between devices: 101 us -> 61.6 us  [body(): rows_t = lax.all_gather(rows_t, (GX, GY), axis=0, tiled=True)]
    all_gather x0 -> x1, blocking collectives: none -> 18.4 us  [body(): rows_t = lax.all_gather(rows_t, ZH, axis=0, tiled=True)]
    unnamed x11 -> x9, local copies, waits for them, and re-layouts: 16.6 us -> 1.87 us
    transpose x0 -> x3, local copies, waits for them, and re-layouts: none -> 13.4 us  [plane_major(): return jnp.swapaxes(w, 0, 1).reshape((d_model,) + tail)]
    convert_element_type x0 -> x2, local copies, waits for them, and re-layouts: none -> 10.6 us  [the longest x1 10.5 us: body(): partial = plane_major(partial.astype(jnp.bfloat16))]
  transfers between devices with their start and end apart: 2 -> 3, of which waited for: 2 -> 3; matrix products, arithmetic and copies ran while one was open for 0% -> 4% of each run, Pallas kernels for 0% -> 0%
where the time goes in v1:
time: 315 us
  waiting for transfers between devices  182 us (58%)
  blocking collectives  50.8 us (16%)
  local copies, waits for them, and re-layouts  37.6 us (12%)
  matrix products  28.5 us (9%)
  between operations  13.2 us (4%)
    reduce_scatter x1, waiting for transfers between devices, body(): lax.psum_scatter(partial, (GX, GY), scatter_dimension=0, tiled=True)  88.5 us
    all_gather x1, waiting for transfers between devices, body(): rows_t = lax.all_gather(rows_t, (GX, GY), axis=0, tiled=True)  61.6 us
    reduce_scatter x1, waiting for transfers between devices, body(): summed = lax.psum_scatter(summed, ZH, scatter_dimension=0, tiled=True)  32 us
    all_gather x1, blocking collectives, body(): rows_t = lax.all_gather(rows_t, ZH, axis=0, tiled=True)  18.4 us
    all_to_all x1, blocking collectives, body(): lax.all_to_all(payload, EXPERT, split_axis=1, concat_axis=1, tiled=True)  17.9 us
    dot_general x1, matrix products, body(): lax.dot_general(down, hidden, (((0,), (1,)), ((), ())), preferred_element...  16.6 us
    all_to_all x1, blocking collectives, body(): lax.all_to_all(summed, EXPERT, split_axis=1, concat_axis=1, tiled=True)  14.5 us
    transpose x3, local copies, waits for them, and re-layouts, plane_major(): return jnp.swapaxes(w, 0, 1).reshape((d_model,) + tail)  13.4 us
  transfers between devices with their start and end apart: 3, of which 3 were waited for; matrix products, arithmetic and copies ran while one was open for 4% of the time, Pallas kernels for 0%

profile of v1, /device:TPU:1, one launch (start us, length us, event | category | flops | bytes accessed | tf_op | source)
XLA Modules:
  0.0 314.6 jit_solution(15060549521055338200)
XLA Ops:
  6.5 0.9 rev.4
  7.4 0.9 copy.55
  10.1 1.1 fusion.5
  12.0 1.8 copy.58
  13.8 17.9 %all_to_all.21 = bf16[200,8,80]{0,2,1:T(8,128)(2,1)} all-to-all(bf16[200,8,80]{0,2,1:T(8,128)(2,1)} %bitcast.49), channel_id=1, replica_groups=mesh['expert'=8,'zh'=2,'x'=4,'y'=4] {'expert'}, dimensions={1} | all-to-all | bytes 512000 | tf_op jit(solution)/shard_map/all_to_all | solution.py:42
  31.7 1.8 copy.59
  33.5 18.4 %all_gather.6 = bf16[384,640]{1,0:T(8,128)(2,1)} all-gather(bf16[192,640]{1,0:T(8,128)(2,1)} %copy.59), channel_id=1, replica_groups=mesh['expert'=8,'zh'=2,'x'=4,'y'=4] {'zh'}, dimensions={0}, use_global_device_ids=true | all-gather | bytes 737280 | tf_op jit(solution)/shard_map/all_gather | solution.py:46
  52.0 1.7 reshape.84
  53.7 1.7 copy.67
  55.4 1.7 reshape.85
  57.1 4.1 %copy.60 = bf16[16,2,192,256]{3,2,1,0:T(8,128)(2,1)} copy(bf16[16,2,192,256]{3,2,0,1:T(8,128)(2,1)} %bitcast.44) | data formatting | bytes 6291456 | tf_op jit(solution)/shard_map/transpose | solution.py:52
  61.2 2.0 copy.61
  63.6 61.6 %all-gather.2.cloned.1.call-done = bf16[6144,640]{1,0:T(8,128)(2,1)} async-done(((bf16[384,640]{1,0:T(8,128)(2,1)}), bf16[6144,640]{1,0:T(8,128)(2,1)}) %all-gather.2.cloned.1.call-update) | async-done | bytes 7864336 | tf_op jit(solution)/shard_map/all_gather | solution.py:47
  125.3 4.5 %select_reduce_fusion.1 = (f32[640]{0:T(1024)S(1)}, f32[640]{0:T(1024)S(1)}) fusion(s32[640]{0:T(1024)S(1)} %reshape.88, pred[8]{0:T(512)(128)(4,1)S(1)} %iota_compare_fusion.6, bf16[6144,640]{1,0:T(8,128)(2,1)} %all-gather.2.cloned.1.call-done, bf16[6144,8]{0,1:T(8,128)(2,1)} %reshape.85), kind=kOutput, calls=%fused_computation.21 | convolution fusion | flops 62938880 | bytes 7970312 | tf_op jit(solution)/shard_map/dot_general | solution.py:55
  129.8 1.0 copy-done.1
  130.8 5.0 %fusion.12 = f32[640,256]{1,0:T(8,128)} fusion(bf16[6144,640]{1,0:T(8,128)(2,1)S(1)} %copy-done.1, bf16[6144,256]{1,0:T(8,128)(2,1)} %bitcast.43), kind=kOutput, calls=%fused_computation.32 | convolution fusion | flops 2013265920 | bytes 11665408 | tf_op jit(solution)/shard_map/dot_general | solution.py:61
  135.7 16.6 %fusion = bf16[6144,640]{0,1:T(8,128)(2,1)} fusion(bf16[1,256,6144]{2,1,0:T(8,128)(2,1)S(1)} %copy-done, bf16[6144,640]{1,0:T(8,128)(2,1)} %all-gather.2.cloned.1.call-done, bf16[6144,256]{1,0:T(8,128)(2,1)} %bitcast.46, f32[640,256]{1,0:T(8,128)} %fusion.12, f32[640]{0:T(1024)S(1)} %fusion.10), kind=kOutput, calls=%fused_computation.1 | convolution fusion | flops 4031610880 | bytes 22678016 | tf_op jit(solution)/shard_map/dot_general | solution.py:66
  152.4 10.5 %copy.63 = bf16[6144,640]{1,0:T(8,128)(2,1)} copy(bf16[6144,640]{0,1:T(8,128)(2,1)} %fusion) | data formatting | bytes 15728640 | tf_op jit(solution)/shard_map/convert_element_type | solution.py:67
  162.9 7.3 %copy.64 = bf16[16,2,192,640]{3,2,1,0:T(8,128)(2,1)} copy(bf16[16,2,192,640]{3,2,0,1:T(8,128)(2,1)} %bitcast.42) | data formatting | bytes 15728640 | tf_op jit(solution)/shard_map/transpose | solution.py:52
  170.2 88.5 %reduce-scatter.3.cloned.1.call-done = bf16[384,640]{1,0:T(8,128)(2,1)} async-done(((bf16[6144,640]{1,0:T(8,128)(2,1)}), bf16[384,640]{1,0:T(8,128)(2,1)}) %reduce-scatter.3.cloned.1.call-update) | async-done | bytes 491536 | tf_op jit(solution)/shard_map/reduce_scatter | solution.py:68
  258.7 32.0 %reduce-scatter.5.cloned.1.call-done = bf16[192,640]{1,0:T(8,128)(2,1)} async-done(((bf16[384,640]{1,0:T(8,128)(2,1)}), bf16[192,640]{1,0:T(8,128)(2,1)}) %reduce-scatter.5.cloned.1.call-update) | async-done | bytes 245776 | tf_op jit(solution)/shard_map/reduce_scatter | solution.py:69
  290.7 1.8 copy.65
  292.5 14.5 %all_to_all.22 = bf16[192,8,80]{0,2,1:T(8,128)(2,1)S(1)} all-to-all(bf16[192,8,80]{0,2,1:T(8,128)(2,1)} %bitcast.50), channel_id=1, replica_groups=mesh['expert'=8,'zh'=2,'x'=4,'y'=4] {'expert'}, dimensions={1} | all-to-all | bytes 491520 | tf_op jit(solution)/shard_map/all_to_all | solution.py:70
  307.1 1.0 convolution_convert_fusion.2
  (28 shorter events, 3.0 us)
Async XLA Ops:
  6.5 129.2 %copy-start = (bf16[1,256,6144]{2,1,0:T(8,128)(2,1)S(1)}, bf16[1,256,6144]{2,1,0:T(8,128)(2,1)}, u32[]{:S(2)}) copy-start(bf16[1,256,6144]{2,1,0:T(8,128)(2,1)} %param.11) | copy-start | bytes 9437188
  6.5 118.7 %all-gather.2.cloned.1.call-start = ((), (), s32[]{:S(2)}) async-start(), calls=%async_computation.4 | async-start | bytes 8355840 | tf_op jit(solution)/shard_map/all_gather | solution.py:47
  51.9 206.7 %reduce-scatter.3.cloned.1.call-start = ((), (), s32[]{:S(2)}) async-start(), calls=%async_computation.5 | async-start | bytes 8355840 | tf_op jit(solution)/shard_map/reduce_scatter | solution.py:68
  57.1 4.1 %copy-start.2 = (bf16[1,6144,256]{2,1,0:T(8,128)(2,1)S(1)}, bf16[1,6144,256]{2,1,0:T(8,128)(2,1)}, u32[]{:S(2)}) copy-start(bf16[1,6144,256]{2,1,0:T(8,128)(2,1)} %param.10) | copy-start | bytes 9437188
  61.2 2.0 copy-start.3
  125.3 5.5 %copy-start.1 = (bf16[6144,640]{1,0:T(8,128)(2,1)S(1)}, bf16[6144,640]{1,0:T(8,128)(2,1)}, u32[]{:S(2)}) copy-start(bf16[6144,640]{1,0:T(8,128)(2,1)} %all-gather.2.cloned.1.call-done) | copy-start | bytes 23592964
  170.2 120.5 %reduce-scatter.5.cloned.1.call-start = ((), (), s32[]{:S(2)}) async-start(), calls=%async_computation.6 | async-start | bytes 737280 | tf_op jit(solution)/shard_map/reduce_scatter | solution.py:69
Sparse Core Ops, SparseCore 0:
  52.1 73.1 all-gather.1
  170.3 88.3 reduce-scatter.2
  261.2 29.4 reduce-scatter.4

commit v2 on v1

v2 whole, which is shorter than its diff:
```python
import jax
import jax.numpy as jnp
from jax import lax
from jax.sharding import Mesh
from jax.sharding import PartitionSpec as P

EXPERT = "expert"
ZH, GX, GY = "zh", "x", "y"
TENSOR = (ZH, GX, GY)
N_CHUNKS = 2


def body(tokens, router_weight, expert_ids, w_gate, w_up, w_down):
    tok_rows, part_width = tokens.shape
    top_count = expert_ids.shape[1]
    n_experts = lax.axis_size(EXPERT)
    n_hi = lax.axis_size(ZH)
    n_plane = lax.axis_size(GX) * lax.axis_size(GY)
    capacity = 5 * tok_rows * top_count // (4 * n_experts)
    slots_all = n_experts * capacity
    d_model = router_weight.shape[0]
    my_expert = lax.axis_index(EXPERT)

    flat_ids = expert_ids.reshape(-1)
    picks = tok_rows * top_count
    expert_hot = (flat_ids[:, None] == jnp.arange(n_experts, dtype=jnp.int32)[None, :]).astype(jnp.float32)
    lower = (jnp.arange(picks)[:, None] > jnp.arange(picks)[None, :]).astype(jnp.float32)
    before = jnp.dot(lower, expert_hot, precision=lax.Precision.HIGHEST)
    slot_pos = jnp.sum(before * expert_hot, axis=1).astype(jnp.int32)
    kept = slot_pos < capacity
    target = flat_ids * capacity + slot_pos
    placed = (target[:, None] == jnp.arange(slots_all, dtype=jnp.int32)[None, :]) & kept[:, None]
    placed = placed.reshape(tok_rows, top_count, slots_all).astype(jnp.float32)
    dispatch = jnp.sum(placed, axis=1).astype(jnp.bfloat16)
    other_id = jnp.flip(expert_ids, axis=1).astype(jnp.float32)
    other_of_slot = jnp.sum(placed * other_id[:, :, None], axis=(0, 1))

    bucket_t = lax.dot_general(
        tokens, dispatch, (((0,), (0,)), ((), ())), preferred_element_type=jnp.float32
    ).astype(jnp.bfloat16)
    meta = jnp.broadcast_to(other_of_slot.astype(jnp.bfloat16)[None, :], (8, slots_all))
    payload = jnp.concatenate([bucket_t, meta], axis=0)
    rows_in = payload.shape[0]
    payload = jnp.swapaxes(payload.reshape(rows_in, n_experts, capacity), 0, 1)
    payload = jnp.broadcast_to(payload[:, None], (n_experts, n_hi, rows_in, capacity))
    payload = payload.reshape(n_experts * n_hi, rows_in, capacity)
    got = lax.all_to_all(payload, (EXPERT, ZH), 0, 0, tiled=True)
    got = got.reshape(n_experts, n_hi, rows_in, capacity)
    other_here = got[:, 0, part_width, :].reshape(slots_all).astype(jnp.int32)
    rows_t = jnp.transpose(got[:, :, :part_width, :], (1, 2, 0, 3)).reshape(n_hi * part_width, slots_all)

    def plane_major(w, axis):
        shape = w.shape
        w = w.reshape(shape[:axis] + (n_hi, n_plane, part_width) + shape[axis + 1 :])
        return jnp.swapaxes(w, axis, axis + 1).reshape(shape)

    router_pm = plane_major(router_weight, 0)
    gate_pm = plane_major(w_gate[0], 0)
    up_pm = plane_major(w_up[0], 0)
    down_pm = plane_major(w_down[0], 1)
    contract_first = (((0,), (0,)), ((), ()))
    expert_col = jnp.arange(n_experts, dtype=jnp.int32)[None, :]

    chunk = slots_all // N_CHUNKS
    sums = []
    ahead = None
    pending = None
    for c in range(N_CHUNKS):
        part = rows_t[:, c * chunk : (c + 1) * chunk]
        if ahead is not None:
            part, _ = lax.optimization_barrier((part, ahead))
        full = lax.all_gather(part, (GX, GY), axis=0, tiled=True)
        ahead = full
        if pending is not None:
            full, pending = lax.optimization_barrier((full, pending))
            sums.append(lax.psum_scatter(pending, (GX, GY), scatter_dimension=1, tiled=True))
        logits = lax.dot_general(full, router_pm, contract_first, preferred_element_type=jnp.float32)
        other = other_here[c * chunk : (c + 1) * chunk]
        own_logit = jnp.sum(jnp.where(expert_col == my_expert, logits, 0.0), axis=1)
        other_logit = jnp.sum(jnp.where(expert_col == other[:, None], logits, 0.0), axis=1)
        weight = jax.nn.sigmoid(own_logit - other_logit).astype(jnp.bfloat16).astype(jnp.float32)
        gate = lax.dot_general(full, gate_pm, contract_first, preferred_element_type=jnp.float32)
        upper = lax.dot_general(full, up_pm, contract_first, preferred_element_type=jnp.float32)
        hidden = (jax.nn.silu(gate) * upper * weight[:, None]).astype(jnp.bfloat16)
        pending = jnp.dot(hidden, down_pm, preferred_element_type=jnp.float32).astype(jnp.bfloat16)
    sums.append(lax.psum_scatter(pending, (GX, GY), scatter_dimension=1, tiled=True))
    summed = jnp.concatenate(sums, axis=0)

    back = summed.reshape(n_experts, capacity, n_hi, part_width)
    back = jnp.swapaxes(back, 1, 2).reshape(n_experts * n_hi, capacity, part_width)
    got = lax.all_to_all(back, (EXPERT, ZH), 0, 0, tiled=True)
    got = got.reshape(n_experts, n_hi, capacity, part_width).astype(jnp.float32)
    returned = jnp.sum(got, axis=1).astype(jnp.bfloat16).reshape(slots_all, part_width)

    combine = dispatch
    mixed = jnp.dot(combine, returned, preferred_element_type=jnp.float32)
    return mixed.astype(jnp.bfloat16)


def solution(mesh):
    n_expert, n_tensor = mesh.devices.shape
    fine = Mesh(mesh.devices.reshape(n_expert, 2, 4, n_tensor // 8), (EXPERT, ZH, GX, GY))
    in_specs = (
        P(EXPERT, TENSOR),
        P(),
        P(EXPERT, None),
        P(EXPERT, None, TENSOR),
        P(EXPERT, None, TENSOR),
        P(EXPERT, TENSOR, None),
    )
    out_specs = P(EXPERT, TENSOR)
    return jax.shard_map(body, mesh=fine, in_specs=in_specs, out_specs=out_specs, check_vma=False)
```

time: 315 us -> 399 us (1.27)
  waiting for transfers between devices: 182 us -> 249 us
  blocking collectives: 50.8 us -> 59.6 us
  matrix products: 28.5 us -> 33.7 us
    unnamed x3 -> x6, waiting for transfers between devices: 0.05 us -> 163 us
    reduce_scatter x2 -> x0, waiting for transfers between devices: 120 us -> none  [the longest x1 88.5 us: body(): lax.psum_scatter(partial, (GX, GY), scatter_dimension=0, tiled=True)]
    all_to_all x2, blocking collectives: 32.4 us -> 59.6 us  [the longest x1 30.1 us: body(): got = lax.all_to_all(payload, (EXPERT, ZH), 0, 0, tiled=True)]
    all_gather x1 -> x2, waiting for transfers between devices: 61.6 us -> 86.5 us  [body(): full = lax.all_gather(part, (GX, GY), axis=0, tiled=True)]
    unnamed x9 -> x24, local copies, waits for them, and re-layouts: 1.87 us -> 22.9 us
    all_gather x1 -> x0, blocking collectives: 18.4 us -> none  [body(): rows_t = lax.all_gather(rows_t, ZH, axis=0, tiled=True)]
    convert_element_type x2 -> x0, local copies, waits for them, and re-layouts: 10.6 us -> none  [the longest x1 10.5 us: body(): partial = plane_major(partial.astype(jnp.bfloat16))]
    dot_general x4 -> x7, matrix products: 27.1 us -> 33.2 us  [the longest x2 18.6 us: body(): jnp.dot(hidden, down_pm, preferred_element_type=jnp.float32)]
  transfers between devices with their start and end apart: 3 -> 4, of which waited for: 3 -> 4; matrix products, arithmetic and copies ran while one was open for 4% -> 10% of each run, Pallas kernels for 0% -> 0%
where the time goes in v2:
time: 399 us; the launch traced here: 398 us
  waiting for transfers between devices  249 us (62%)
  blocking collectives  59.6 us (15%)
  local copies, waits for them, and re-layouts  39.2 us (10%)
  matrix products  33.7 us (8%)
  between operations  13.4 us (3%)
    unnamed x6, waiting for transfers between devices  163 us
    all_gather x2, waiting for transfers between devices, body(): full = lax.all_gather(part, (GX, GY), axis=0, tiled=True)  86.5 us
    all_to_all x1, blocking collectives, body(): got = lax.all_to_all(payload, (EXPERT, ZH), 0, 0, tiled=True)  30.1 us
    all_to_all x1, blocking collectives, body(): got = lax.all_to_all(back, (EXPERT, ZH), 0, 0, tiled=True)  29.5 us
    unnamed x24, local copies, waits for them, and re-layouts  22.9 us
    dot_general x2, matrix products, body(): jnp.dot(hidden, down_pm, preferred_element_type=jnp.float32)  18.6 us
    dot_general x2, matrix products, body(): lax.dot_general(full, gate_pm, contract_first, preferred_element_type=jnp...  8.95 us
  transfers between devices with their start and end apart: 4, of which 4 were waited for; matrix products, arithmetic and copies ran while one was open for 10% of the time, Pallas kernels for 0%

profile of v2, /device:TPU:1, one launch (start us, length us, event | category | flops | bytes accessed | tf_op | source)
XLA Modules:
  0.0 397.8 jit_solution(14892087839511930611)
XLA Ops:
  11.2 30.1 %all_to_all.10 = bf16[16,200,80]{1,2,0:T(8,128)(2,1)S(1)} all-to-all(bf16[16,200,80]{1,2,0:T(8,128)(2,1)S(1)} %bitcast.70), channel_id=1, replica_groups=mesh['expert'=8,'zh'=2,'x'=4,'y'=4] {'expert','zh'}, dimensions={0} | all-to-all | bytes 1024000 | tf_op jit(solution)/shard_map/all_to_all | solution.py:47
  42.1 1.4 copy.73
  43.5 2.8 reshape.109
  46.3 1.9 fusion.30
  48.3 55.9 %all-gather.3.cloned.1.call-done = bf16[6144,320]{0,1:T(8,128)(2,1)} async-done(((bf16[384,320]{0,1:T(8,128)(2,1)}), bf16[6144,320]{0,1:T(8,128)(2,1)}) %all-gather.3.cloned.1.call-update) | async-done | bytes 3932176 | tf_op jit(solution)/shard_map/all_gather | solution.py:72
  106.6 1.8 copy.74
  108.4 4.7 %copy.77 = bf16[1,256,6144]{1,2,0:T(8,128)(2,1)} copy(bf16[1,256,6144]{2,1,0:T(8,128)(2,1)} %param.11) | data formatting | bytes 6291456 | tf_op args[5]
  113.1 2.2 copy.78
  116.0 2.0 copy.75
  118.0 1.0 slice_convert_fusion
  119.4 3.5 select_reduce_fusion.3
  123.0 3.8 fusion.31
  126.8 9.3 %convolution_convert_fusion.1 = bf16[320,6144]{1,0:T(8,128)(2,1)} fusion(bf16[256,6144]{0,1:T(8,128)(2,1)S(1)} %bitcast.57, bf16[6144,320]{0,1:T(8,128)(2,1)} %all-gather.3.cloned.1.call-done, bf16[6144,256]{1,0:T(8,128)(2,1)} %bitcast.59, f32[320,256]{1,0:T(8,128)} %fusion.31, f32[320]{0:T(512)S(1)} %fusion.27), kind=kOutput, calls=%fused_computation.1 | convolution fusion | flops 2015805440 | bytes 14484736 | tf_op jit(solution)/shard_map/dot_general | solution.py:85
  136.1 30.5 %all-gather.5.cloned.1.call-done = bf16[6144,320]{0,1:T(8,128)(2,1)} async-done(((bf16[384,320]{0,1:T(8,128)(2,1)}), bf16[6144,320]{0,1:T(8,128)(2,1)}) %all-gather.5.cloned.1.call-update) | async-done | bytes 3932176 | tf_op jit(solution)/shard_map/all_gather | solution.py:72
  166.7 5.1 %fusion.32 = f32[320,256]{1,0:T(8,128)} fusion(bf16[6144,320]{0,1:T(8,128)(2,1)} %all-gather.5.cloned.1.call-done, bf16[6144,256]{1,0:T(8,128)(2,1)} %bitcast.69), kind=kOutput, calls=%fused_computation.63 | convolution fusion | flops 1006632960 | bytes 7405568 | tf_op jit(solution)/shard_map/dot_general | solution.py:82
  171.8 1.1 select_reduce_fusion.1
  173.0 9.2 %convolution_convert_fusion = bf16[320,6144]{1,0:T(8,128)(2,1)} fusion(bf16[256,6144]{0,1:T(8,128)(2,1)S(1)} %bitcast.58, bf16[6144,320]{0,1:T(8,128)(2,1)} %all-gather.5.cloned.1.call-done, bf16[6144,256]{1,0:T(8,128)(2,1)} %bitcast.60, f32[320,256]{1,0:T(8,128)} %fusion.32, f32[320]{0:T(512)S(1)} %fusion.26), kind=kOutput, calls=%fused_computation | convolution fusion | flops 2015805440 | bytes 14484736 | tf_op jit(solution)/shard_map/dot_general | solution.py:85
  182.2 6.4 %copy.82 = bf16[320,6144]{0,1:T(8,128)(2,1)} copy(bf16[320,6144]{1,0:T(8,128)(2,1)} %convolution_convert_fusion) | data formatting | bytes 7864320
  188.6 6.5 %copy.80 = bf16[320,6144]{0,1:T(8,128)(2,1)} copy(bf16[320,6144]{1,0:T(8,128)(2,1)} %convolution_convert_fusion.1) | data formatting | bytes 7864320
  195.1 76.8 %reduce-scatter.9.cloned.1.call-done = bf16[384,320]{1,0:T(8,128)(2,1)} async-done(((bf16[6144,320]{1,0:T(8,128)(2,1)}), bf16[384,320]{1,0:T(8,128)(2,1)}) %reduce-scatter.9.cloned.1.call-update) | async-done | bytes 245776
  272.0 1.1 copy.83
  273.1 85.9 %reduce-scatter.7.cloned.1.call-done = bf16[384,320]{1,0:T(8,128)(2,1)} async-done(((bf16[6144,320]{1,0:T(8,128)(2,1)}), bf16[384,320]{1,0:T(8,128)(2,1)}) %reduce-scatter.7.cloned.1.call-update) | async-done | bytes 245776
  359.0 1.1 copy.81
  360.7 29.5 %all_to_all.11 = bf16[16,80,192]{2,1,0:T(8,128)(2,1)S(1)} all-to-all(bf16[16,80,192]{2,1,0:T(8,128)(2,1)S(1)} %bitcast.72), channel_id=1, replica_groups=mesh['expert'=8,'zh'=2,'x'=4,'y'=4] {'expert','zh'}, dimensions={0} | all-to-all | bytes 983040 | tf_op jit(solution)/shard_map/all_to_all | solution.py:91
  (57 shorter events, 10.4 us)
Async XLA Ops:
  6.5 4.1 %copy-start = (bf16[256,192]{0,1:T(8,128)(2,1)S(1)}, bf16[256,192]{0,1:T(8,128)(2,1)}, u32[]{:S(2)}) copy-start(bf16[256,192]{0,1:T(8,128)(2,1)} %param.6) | copy-start | bytes 294916
  6.5 97.7 %all-gather.3.cloned.1.call-start = ((), (), s32[]{:S(2)}) async-start(), calls=%async_computation.4 | async-start | bytes 4177920 | tf_op jit(solution)/shard_map/all_gather | solution.py:72
  9.9 0.7 copy-start.6
  11.2 93.3 %copy-start.8 = (bf16[6144,8]{0,1:T(8,128)(2,1)S(1)}, bf16[6144,8]{0,1:T(8,128)(2,1)}, u32[]{:S(2)}) copy-start(bf16[6144,8]{0,1:T(8,128)(2,1)} %param.7) | copy-start | bytes 294916
  41.3 0.8 copy-start.3
  41.3 65.3 %copy-start.4 = (bf16[1,6144,256]{2,1,0:T(8,128)(2,1)S(1)}, bf16[1,6144,256]{2,1,0:T(8,128)(2,1)}, u32[]{:S(2)}) copy-start(bf16[1,6144,256]{2,1,0:T(8,128)(2,1)} %param.9) | copy-start | bytes 9437188
  48.2 118.4 %all-gather.5.cloned.1.call-start = ((), (), s32[]{:S(2)}) async-start(), calls=%async_computation.5 | async-start | bytes 4177920 | tf_op jit(solution)/shard_map/all_gather | solution.py:72
  104.3 167.7 %reduce-scatter.9.cloned.1.call-start = ((), (), s32[]{:S(2)}) async-start(), calls=%async_computation.7 | async-start | bytes 5013504
  113.1 2.8 copy-start.5
  119.4 3.6 copy-start.2
  166.7 5.1 %copy-start.1 = (bf16[6144,320]{0,1:T(8,128)(2,1)S(1)}, bf16[6144,320]{0,1:T(8,128)(2,1)}, u32[]{:S(2)}) copy-start(bf16[6144,320]{0,1:T(8,128)(2,1)} %all-gather.5.cloned.1.call-done) | copy-start | bytes 11796484
  188.6 170.4 %reduce-scatter.7.cloned.1.call-start = ((), (), s32[]{:S(2)}) async-start(), calls=%async_computation.6 | async-start | bytes 5013504
  273.1 117.2 %copy-start.7 = (bf16[256,640]{1,0:T(8,128)(2,1)S(1)}, bf16[256,640]{1,0:T(8,128)(2,1)}, u32[]{:S(2)}) copy-start(bf16[256,640]{1,0:T(8,128)(2,1)} %copy-done.6) | copy-start | bytes 983044
Sparse Core Ops, SparseCore 0:
  48.4 55.8 all-gather.2
  106.6 59.9 all-gather.4
  188.7 83.2 reduce-scatter.8
  275.5 83.5 reduce-scatter.6

commit v3 on v2

--- a/solution.py
+++ b/solution.py
@@ -7,7 +7,6 @@
 EXPERT = "expert"
 ZH, GX, GY = "zh", "x", "y"
 TENSOR = (ZH, GX, GY)
-N_CHUNKS = 2
 
 
 def body(tokens, router_weight, expert_ids, w_gate, w_up, w_down):
@@ -61,30 +60,16 @@
     contract_first = (((0,), (0,)), ((), ()))
     expert_col = jnp.arange(n_experts, dtype=jnp.int32)[None, :]
 
-    chunk = slots_all // N_CHUNKS
-    sums = []
-    ahead = None
-    pending = None
-    for c in range(N_CHUNKS):
-        part = rows_t[:, c * chunk : (c + 1) * chunk]
-        if ahead is not None:
-            part, _ = lax.optimization_barrier((part, ahead))
-        full = lax.all_gather(part, (GX, GY), axis=0, tiled=True)
-        ahead = full
-        if pending is not None:
-            full, pending = lax.optimization_barrier((full, pending))
-            sums.append(lax.psum_scatter(pending, (GX, GY), scatter_dimension=1, tiled=True))
-        logits = lax.dot_general(full, router_pm, contract_first, preferred_element_type=jnp.float32)
-        other = other_here[c * chunk : (c + 1) * chunk]
-        own_logit = jnp.sum(jnp.where(expert_col == my_expert, logits, 0.0), axis=1)
-        other_logit = jnp.sum(jnp.where(expert_col == other[:, None], logits, 0.0), axis=1)
-        weight = jax.nn.sigmoid(own_logit - other_logit).astype(jnp.bfloat16).astype(jnp.float32)
-        gate = lax.dot_general(full, gate_pm, contract_first, preferred_element_type=jnp.float32)
-        upper = lax.dot_general(full, up_pm, contract_first, preferred_element_type=jnp.float32)
-        hidden = (jax.nn.silu(gate) * upper * weight[:, None]).astype(jnp.bfloat16)
-        pending = jnp.dot(hidden, down_pm, preferred_element_type=jnp.float32).astype(jnp.bfloat16)
-    sums.append(lax.psum_scatter(pending, (GX, GY), scatter_dimension=1, tiled=True))
-    summed = jnp.concatenate(sums, axis=0)
+    full = lax.all_gather(rows_t, (GX, GY), axis=0, tiled=True)
+    logits = lax.dot_general(full, router_pm, contract_first, preferred_element_type=jnp.float32)
+    own_logit = jnp.sum(jnp.where(expert_col == my_expert, logits, 0.0), axis=1)
+    other_logit = jnp.sum(jnp.where(expert_col == other_here[:, None], logits, 0.0), axis=1)
+    weight = jax.nn.sigmoid(own_logit - other_logit).astype(jnp.bfloat16).astype(jnp.float32)
+    gate = lax.dot_general(full, gate_pm, contract_first, preferred_element_type=jnp.float32)
+    upper = lax.dot_general(full, up_pm, contract_first, preferred_element_type=jnp.float32)
+    hidden = (jax.nn.silu(gate) * upper * weight[:, None]).astype(jnp.bfloat16)
+    partial = jnp.dot(hidden, down_pm, preferred_element_type=jnp.float32).astype(jnp.bfloat16)
+    summed = lax.psum_scatter(partial, (GX, GY), scatter_dimension=1, tiled=True)
 
     back = summed.reshape(n_experts, capacity, n_hi, part_width)
     back = jnp.swapaxes(back, 1, 2).reshape(n_experts * n_hi, capacity, part_width)

time: 399 us -> 285 us (0.71)
  waiting for transfers between devices: 249 us -> 152 us
  local copies, waits for them, and re-layouts: 39.2 us -> 30.9 us
  matrix products: 33.7 us -> 25.8 us
    unnamed x6 -> x3, waiting for transfers between devices: 163 us -> 89.4 us
    all_gather x2 -> x1, waiting for transfers between devices: 86.5 us -> 62.9 us  [body(): full = lax.all_gather(rows_t, (GX, GY), axis=0, tiled=True)]
    dot_general x2 -> x1, matrix products: 18.6 us -> 13.7 us  [body(): jnp.dot(hidden, down_pm, preferred_element_type=jnp.float32)]
    unnamed x24 -> x22, local copies, waits for them, and re-layouts: 22.9 us -> 18.4 us
    dot_general x2 -> x1, matrix products: 8.95 us -> 5.09 us  [body(): lax.dot_general(full, gate_pm, contract_first, preferred_element_type=jnp...]
  transfers between devices with their start and end apart: 4 -> 2, of which waited for: 4 -> 2; matrix products, arithmetic and copies ran while one was open for 10% -> 4% of each run, Pallas kernels for 0% -> 0%
where the time goes in v3:
time: 285 us
  waiting for transfers between devices  152 us (53%)
  blocking collectives  59.2 us (21%)
  local copies, waits for them, and re-layouts  30.9 us (11%)
  matrix products  25.8 us (9%)
  between operations  13.6 us (5%)
    unnamed x3, waiting for transfers between devices  89.4 us
    all_gather x1, waiting for transfers between devices, body(): full = lax.all_gather(rows_t, (GX, GY), axis=0, tiled=True)  62.9 us
    all_to_all x1, blocking collectives, body(): got = lax.all_to_all(payload, (EXPERT, ZH), 0, 0, tiled=True)  30.2 us
    all_to_all x1, blocking collectives, body(): got = lax.all_to_all(back, (EXPERT, ZH), 0, 0, tiled=True)  29 us
    unnamed x22, local copies, waits for them, and re-layouts  18.4 us
    dot_general x1, matrix products, body(): jnp.dot(hidden, down_pm, preferred_element_type=jnp.float32)  13.7 us
    transpose x3, local copies, waits for them, and re-layouts, plane_major(): return jnp.swapaxes(w, axis, axis + 1).reshape(shape)  5.9 us
  transfers between devices with their start and end apart: 2, of which 2 were waited for; matrix products, arithmetic and copies ran while one was open for 4% of the time, Pallas kernels for 0%

profile of v3, /device:TPU:1, one launch (start us, length us, event | category | flops | bytes accessed | tf_op | source)
XLA Modules:
  0.0 284.6 jit_solution(13920837948324363582)
XLA Ops:
  6.5 0.8 rev.4
  7.3 0.8 copy.69
  8.8 0.7 multiply_add_fusion
  9.5 0.4 convert_reduce_fusion
  9.9 0.7 copy-done.6
  11.2 30.2 %all_to_all.10 = bf16[16,200,80]{1,2,0:T(8,128)(2,1)S(1)} all-to-all(bf16[16,200,80]{1,2,0:T(8,128)(2,1)S(1)} %bitcast.57), channel_id=1, replica_groups=mesh['expert'=8,'zh'=2,'x'=4,'y'=4] {'expert','zh'}, dimensions={0} | all-to-all | bytes 1024000 | tf_op jit(solution)/shard_map/all_to_all | solution.py:46
  41.4 0.8 copy-done.2
  42.3 1.3 copy.73
  43.6 2.8 %reshape.100 = bf16[384,640]{0,1:T(8,128)(2,1)} reshape(bf16[2,192,8,80]{1,0,3,2:T(2,128)(2,1)} %copy.73) | data formatting | bytes 983040 | tf_op jit(solution)/shard_map/reshape | solution.py:49
  47.3 2.0 copy.74
  49.2 1.1 copy-done.4
  50.3 2.1 copy.75
  52.4 3.2 %copy.77 = bf16[1,256,6144]{1,2,0:T(8,128)(2,1)S(1)} copy(bf16[1,256,6144]{2,1,0:T(8,128)(2,1)} %param.11) | data formatting | bytes 6291456 | tf_op args[5]
  55.5 1.9 copy.78
  57.4 1.2 convert_reduce_fusion.1
  58.7 62.9 %all-gather.2.cloned.1.call-done = bf16[6144,640]{0,1:T(8,128)(2,1)} async-done(((bf16[384,640]{0,1:T(8,128)(2,1)}), bf16[6144,640]{0,1:T(8,128)(2,1)}) %all-gather.2.cloned.1.call-update) | async-done | bytes 7864336 | tf_op jit(solution)/shard_map/all_gather | solution.py:63
  121.6 5.5 %select_reduce_fusion.1 = (f32[640]{0:T(1024)S(1)}, f32[640]{0:T(1024)S(1)}) fusion(s32[640]{0:T(1024)S(1)} %reshape.110, pred[8]{0:T(512)(128)(4,1)S(1)} %iota_compare_fusion.6, bf16[6144,640]{0,1:T(8,128)(2,1)} %all-gather.2.cloned.1.call-done, bf16[6144,8]{0,1:T(8,128)(2,1)S(1)} %reshape.104), kind=kOutput, calls=%fused_computation.28 | convolution fusion | flops 62938880 | bytes 7970312 | tf_op jit(solution)/shard_map/dot_general | solution.py:64
  127.2 5.1 %fusion.17 = f32[640,256]{1,0:T(8,128)} fusion(bf16[6144,640]{0,1:T(8,128)(2,1)S(1)} %copy-done.1, bf16[6144,256]{1,0:T(8,128)(2,1)} %bitcast.56), kind=kOutput, calls=%fused_computation.39 | convolution fusion | flops 2013265920 | bytes 11665408 | tf_op jit(solution)/shard_map/dot_general | solution.py:68
  132.3 13.7 %convolution_convert_fusion = bf16[640,6144]{1,0:T(8,128)(2,1)} fusion(bf16[256,6144]{0,1:T(8,128)(2,1)} %bitcast.55, bf16[6144,640]{0,1:T(8,128)(2,1)} %all-gather.2.cloned.1.call-done, bf16[6144,256]{1,0:T(8,128)(2,1)S(1)} %bitcast.54, f32[640,256]{1,0:T(8,128)} %fusion.17, f32[640]{0:T(1024)S(1)} %fusion.15), kind=kOutput, calls=%fused_computation | convolution fusion | flops 4031610880 | bytes 22678016 | tf_op jit(solution)/shard_map/dot_general | solution.py:71
  146.0 10.5 %copy.80 = bf16[640,6144]{0,1:T(8,128)(2,1)} copy(bf16[640,6144]{1,0:T(8,128)(2,1)} %convolution_convert_fusion) | data formatting | bytes 15728640
  156.5 89.4 %reduce-scatter.4.cloned.1.call-done = bf16[384,640]{1,0:T(8,128)(2,1)} async-done(((bf16[6144,640]{1,0:T(8,128)(2,1)}), bf16[384,640]{1,0:T(8,128)(2,1)}) %reduce-scatter.4.cloned.1.call-update) | async-done | bytes 491536
  245.9 1.3 copy.81
  247.6 29.0 %all_to_all.11 = bf16[16,80,192]{2,1,0:T(8,128)(2,1)S(1)} all-to-all(bf16[16,80,192]{2,1,0:T(8,128)(2,1)S(1)} %bitcast.59), channel_id=1, replica_groups=mesh['expert'=8,'zh'=2,'x'=4,'y'=4] {'expert','zh'}, dimensions={0} | all-to-all | bytes 983040 | tf_op jit(solution)/shard_map/all_to_all | solution.py:76
  276.8 1.0 convolution_convert_fusion.2
  (41 shorter events, 2.6 us)
Async XLA Ops:
  6.5 4.1 %copy-start = (bf16[256,192]{0,1:T(8,128)(2,1)S(1)}, bf16[256,192]{0,1:T(8,128)(2,1)}, u32[]{:S(2)}) copy-start(bf16[256,192]{0,1:T(8,128)(2,1)} %param.6) | copy-start | bytes 294916
  6.5 115.1 %all-gather.2.cloned.1.call-start = ((), (), s32[]{:S(2)}) async-start(), calls=%async_computation.3 | async-start | bytes 8355840 | tf_op jit(solution)/shard_map/all_gather | solution.py:63
  9.9 0.7 copy-start.6
  11.1 35.6 %copy-start.8 = (bf16[6144,8]{0,1:T(8,128)(2,1)S(1)}, bf16[6144,8]{0,1:T(8,128)(2,1)}, u32[]{:S(2)}) copy-start(bf16[6144,8]{0,1:T(8,128)(2,1)} %param.7) | copy-start | bytes 294916
  11.2 36.0 %copy-start.3 = (bf16[1,6144,256]{2,1,0:T(8,128)(2,1)S(1)}, bf16[1,6144,256]{2,1,0:T(8,128)(2,1)}, u32[]{:S(2)}) copy-start(bf16[1,6144,256]{2,1,0:T(8,128)(2,1)} %param.9) | copy-start | bytes 9437188
  41.4 0.8 copy-start.2
  46.5 199.4 %reduce-scatter.4.cloned.1.call-start = ((), (), s32[]{:S(2)}) async-start(), calls=%async_computation.4 | async-start | bytes 8355840
  47.3 3.0 %copy-start.4 = (bf16[1,6144,256]{2,1,0:T(8,128)(2,1)S(1)}, bf16[1,6144,256]{2,1,0:T(8,128)(2,1)}, u32[]{:S(2)}) copy-start(bf16[1,6144,256]{2,1,0:T(8,128)(2,1)} %param.10) | copy-start | bytes 9437188
  121.6 5.6 %copy-start.1 = (bf16[6144,640]{0,1:T(8,128)(2,1)S(1)}, bf16[6144,640]{0,1:T(8,128)(2,1)}, u32[]{:S(2)}) copy-start(bf16[6144,640]{0,1:T(8,128)(2,1)} %all-gather.2.cloned.1.call-done) | copy-start | bytes 23592964
  127.2 5.1 %copy-start.5 = (bf16[16,2,192,256]{3,2,1,0:T(8,128)(2,1)S(1)}, bf16[16,2,192,256]{3,2,1,0:T(8,128)(2,1)}, u32[]{:S(2)}) copy-start(bf16[16,2,192,256]{3,2,1,0:T(8,128)(2,1)} %copy.75) | copy-start | bytes 9437188
  156.5 120.3 %copy-start.7 = (bf16[256,640]{1,0:T(8,128)(2,1)S(1)}, bf16[256,640]{1,0:T(8,128)(2,1)}, u32[]{:S(2)}) copy-start(bf16[256,640]{1,0:T(8,128)(2,1)} %copy-done.6) | copy-start | bytes 983044
Sparse Core Ops, SparseCore 0:
  46.6 74.9 all-gather.1
  156.6 89.2 reduce-scatter.3

commit v4 on v3

--- a/solution.py
+++ b/solution.py
@@ -1,12 +1,30 @@
 import jax
 import jax.numpy as jnp
 from jax import lax
+from jax.experimental import pallas as pl
 from jax.sharding import Mesh
 from jax.sharding import PartitionSpec as P
 
 EXPERT = "expert"
 ZH, GX, GY = "zh", "x", "y"
 TENSOR = (ZH, GX, GY)
+
+
+def _down_kernel(a_ref, b_ref, o_ref):
+    o_ref[...] = jnp.dot(a_ref[...], b_ref[...], preferred_element_type=jnp.float32).astype(o_ref.dtype)
+
+
+def down_project(down_t, hidden_t):
+    d_rows, ff = down_t.shape
+    rows = hidden_t.shape[1]
+    block = 768
+    return pl.pallas_call(
+        _down_kernel,
+        grid=(d_rows // block,),
+        in_specs=[pl.BlockSpec((block, ff), lambda i: (i, 0)), pl.BlockSpec((ff, rows), lambda i: (0, 0))],
+        out_specs=pl.BlockSpec((block, rows), lambda i: (i, 0)),
+        out_shape=jax.ShapeDtypeStruct((d_rows, rows), jnp.bfloat16),
+    )(down_t, hidden_t)
 
 
 def body(tokens, router_weight, expert_ids, w_gate, w_up, w_down):
@@ -53,32 +71,35 @@
         w = w.reshape(shape[:axis] + (n_hi, n_plane, part_width) + shape[axis + 1 :])
         return jnp.swapaxes(w, axis, axis + 1).reshape(shape)
 
-    router_pm = plane_major(router_weight, 0)
-    gate_pm = plane_major(w_gate[0], 0)
-    up_pm = plane_major(w_up[0], 0)
-    down_pm = plane_major(w_down[0], 1)
+    ff_dev = w_gate.shape[2]
+    fused_w = jnp.concatenate(
+        [plane_major(w_gate[0], 0), plane_major(w_up[0], 0), plane_major(router_weight, 0)], axis=1
+    )
+    down_t = jnp.swapaxes(plane_major(w_down[0], 1), 0, 1)
     contract_first = (((0,), (0,)), ((), ()))
     expert_col = jnp.arange(n_experts, dtype=jnp.int32)[None, :]
 
     full = lax.all_gather(rows_t, (GX, GY), axis=0, tiled=True)
-    logits = lax.dot_general(full, router_pm, contract_first, preferred_element_type=jnp.float32)
+    fused = lax.dot_general(full, fused_w, contract_first, preferred_element_type=jnp.float32)
+    gate = fused[:, :ff_dev]
+    upper = fused[:, ff_dev : 2 * ff_dev]
+    logits = fused[:, 2 * ff_dev :]
     own_logit = jnp.sum(jnp.where(expert_col == my_expert, logits, 0.0), axis=1)
     other_logit = jnp.sum(jnp.where(expert_col == other_here[:, None], logits, 0.0), axis=1)
     weight = jax.nn.sigmoid(own_logit - other_logit).astype(jnp.bfloat16).astype(jnp.float32)
-    gate = lax.dot_general(full, gate_pm, contract_first, preferred_element_type=jnp.float32)
-    upper = lax.dot_general(full, up_pm, contract_first, preferred_element_type=jnp.float32)
     hidden = (jax.nn.silu(gate) * upper * weight[:, None]).astype(jnp.bfloat16)
-    partial = jnp.dot(hidden, down_pm, preferred_element_type=jnp.float32).astype(jnp.bfloat16)
-    summed = lax.psum_scatter(partial, (GX, GY), scatter_dimension=1, tiled=True)
+    partial = down_project(down_t, hidden.T)
+    summed = lax.psum_scatter(partial, (GX, GY), scatter_dimension=0, tiled=True)
 
-    back = summed.reshape(n_experts, capacity, n_hi, part_width)
-    back = jnp.swapaxes(back, 1, 2).reshape(n_experts * n_hi, capacity, part_width)
+    back = summed.reshape(n_hi, part_width, n_experts, capacity)
+    back = jnp.transpose(back, (2, 0, 1, 3)).reshape(n_experts * n_hi, part_width, capacity)
     got = lax.all_to_all(back, (EXPERT, ZH), 0, 0, tiled=True)
-    got = got.reshape(n_experts, n_hi, capacity, part_width).astype(jnp.float32)
-    returned = jnp.sum(got, axis=1).astype(jnp.bfloat16).reshape(slots_all, part_width)
+    got = got.reshape(n_experts, n_hi, part_width, capacity).astype(jnp.float32)
+    returned = jnp.sum(got, axis=1).astype(jnp.bfloat16)
+    returned = jnp.swapaxes(returned, 0, 1).reshape(part_width, slots_all)
 
     combine = dispatch
-    mixed = jnp.dot(combine, returned, preferred_element_type=jnp.float32)
+    mixed = lax.dot_general(combine, returned, (((1,), (1,)), ((), ())), preferred_element_type=jnp.float32)
     return mixed.astype(jnp.bfloat16)
 
 

time: 285 us -> 270 us (0.947)
  matrix products: 25.8 us -> 12.2 us
  local copies, waits for them, and re-layouts: 30.9 us -> 22 us
  Pallas kernels: 0 us -> 8.66 us
    reduce_scatter x0 -> x1, waiting for transfers between devices: none -> 89.5 us  [body(): lax.psum_scatter(partial, (GX, GY), scatter_dimension=0, tiled=True)]
    unnamed x3 -> x2, waiting for transfers between devices: 89.4 us -> 0.03 us
    dot_general x4 -> x2, matrix products: 25.3 us -> 11.7 us  [the longest x1 10.7 us: body(): lax.dot_general(full, fused_w, contract_first, preferred_element_type=jnp...]
    unnamed x22 -> x16, local copies, waits for them, and re-layouts: 18.4 us -> 6.8 us
    pallas_call x0 -> x1, Pallas kernels: none -> 8.66 us  [down_project(): pl.pallas_call(_down_kernel, grid=(d_rows // block,), in_specs=[pl.BlockS...]
  transfers between devices with their start and end apart: 2 -> 2, of which waited for: 2 -> 2; matrix products, arithmetic and copies ran while one was open for 4% -> 5% of each run, Pallas kernels for 0% -> 0%
where the time goes in v4:
time: 270 us
  waiting for transfers between devices  151 us (56%)
  blocking collectives  58.9 us (22%)
  local copies, waits for them, and re-layouts  22 us (8%)
  between operations  13.6 us (5%)
  matrix products  12.2 us (5%)
  Pallas kernels  8.66 us (3%)
  other arithmetic  3.55 us (1%)
    reduce_scatter x1, waiting for transfers between devices, body(): lax.psum_scatter(partial, (GX, GY), scatter_dimension=0, tiled=True)  89.5 us
    all_gather x1, waiting for transfers between devices, body(): full = lax.all_gather(rows_t, (GX, GY), axis=0, tiled=True)  61.5 us
    all_to_all x1, blocking collectives, body(): got = lax.all_to_all(payload, (EXPERT, ZH), 0, 0, tiled=True)  29.9 us
    all_to_all x1, blocking collectives, body(): got = lax.all_to_all(back, (EXPERT, ZH), 0, 0, tiled=True)  29 us
    dot_general x1, matrix products, body(): lax.dot_general(full, fused_w, contract_first, preferred_element_type=jnp...  10.7 us
    pallas_call x1, Pallas kernels, down_project(): pl.pallas_call(_down_kernel, grid=(d_rows // block,), in_specs=[pl.BlockS...  8.66 us
    unnamed x16, local copies, waits for them, and re-layouts  6.8 us
    transpose x3, local copies, waits for them, and re-layouts, plane_major(): return jnp.swapaxes(w, axis, axis + 1).reshape(shape)  5.87 us
  transfers between devices with their start and end apart: 2, of which 2 were waited for; matrix products, arithmetic and copies ran while one was open for 5% of the time, Pallas kernels for 0%

profile of v4, /device:TPU:1, one launch (start us, length us, event | category | flops | bytes accessed | tf_op | source)
XLA Modules:
  0.0 269.9 jit_solution(2619796616905328749)
XLA Ops:
  6.5 0.8 rev.4
  7.3 0.8 copy.53
  8.8 0.7 multiply_add_fusion
  9.5 0.4 convert_reduce_fusion
  9.9 0.7 copy-done.4
  11.2 29.9 %all_to_all.10 = bf16[16,200,80]{1,2,0:T(8,128)(2,1)S(1)} all-to-all(bf16[16,200,80]{1,2,0:T(8,128)(2,1)S(1)} %bitcast.55), channel_id=1, replica_groups=mesh['expert'=8,'zh'=2,'x'=4,'y'=4] {'expert','zh'}, dimensions={0} | all-to-all | bytes 1024000 | tf_op jit(solution)/shard_map/all_to_all | solution.py:64
  41.1 0.8 copy-done.1
  42.0 1.3 copy.59
  43.3 2.8 %reshape.101 = bf16[384,640]{0,1:T(8,128)(2,1)} reshape(bf16[2,192,8,80]{1,0,3,2:T(2,128)(2,1)} %copy.59) | data formatting | bytes 983040 | tf_op jit(solution)/shard_map/reshape | solution.py:67
  46.6 1.6 copy.66
  48.2 1.8 copy.60
  50.0 1.2 copy-done.3
  51.2 2.1 copy.61
  53.3 3.2 %copy.56 = bf16[1,256,6144]{1,2,0:T(8,128)(2,1)S(1)} copy(bf16[1,256,6144]{2,1,0:T(8,128)(2,1)} %param.11) | data formatting | bytes 6291456 | tf_op args[5]
  56.5 1.9 copy.57
  58.5 1.2 convert_reduce_fusion.1
  59.8 61.5 %all-gather.2.cloned.1.call-done = bf16[6144,640]{0,1:T(8,128)(2,1)} async-done(((bf16[384,640]{0,1:T(8,128)(2,1)}), bf16[6144,640]{0,1:T(8,128)(2,1)}) %all-gather.2.cloned.1.call-update) | async-done | bytes 7864336 | tf_op jit(solution)/shard_map/all_gather | solution.py:82
  121.3 10.7 %fusion = f32[640,520]{0,1:T(8,128)S(1)} fusion(bf16[6144,640]{0,1:T(8,128)(2,1)} %all-gather.2.cloned.1.call-done, bf16[6144,8]{1,0:T(8,128)(2,1)} %bitcast.58, bf16[6144,256]{1,0:T(8,128)(2,1)} %bitcast.54, bf16[6144,256]{1,0:T(8,128)(2,1)} %bitcast.53), kind=kOutput, calls=%fused_computation | convolution fusion | flops 4108615680 | bytes 15585280 | tf_op jit(solution)/shard_map/dot_general | solution.py:83
  132.1 1.0 fusion.11.b_ref
  133.1 8.7 %shard_map.64 = bf16[6144,640]{1,0:T(8,128)(2,1)} custom-call(bf16[6144,256]{1,0:T(8,128)(2,1)} %bitcast.48, bf16[256,640]{1,0:T(8,128)(2,1)} %fusion.11.b_ref), custom_call_target="tpu_custom_call" | custom-call | tf_op jit(solution)/shard_map/pallas_call | solution.py:21
  141.8 89.5 %reduce-scatter.2.cloned.1.call-done = bf16[384,640]{1,0:T(8,128)(2,1)} async-done(((bf16[6144,640]{1,0:T(8,128)(2,1)}), bf16[384,640]{1,0:T(8,128)(2,1)}) %reduce-scatter.2.cloned.1.call-update) | async-done | bytes 491536 | tf_op jit(solution)/shard_map/reduce_scatter | solution.py:92
  231.3 1.3 copy.64
  233.0 29.0 %all_to_all.11 = bf16[16,192,80]{1,2,0:T(8,128)(2,1)S(1)} all-to-all(bf16[16,192,80]{1,2,0:T(8,128)(2,1)S(1)} %bitcast.57), channel_id=1, replica_groups=mesh['expert'=8,'zh'=2,'x'=4,'y'=4] {'expert','zh'}, dimensions={0} | all-to-all | bytes 983040 | tf_op jit(solution)/shard_map/all_to_all | solution.py:96
  262.1 1.0 convolution_convert_fusion.1
  (37 shorter events, 2.3 us)
Async XLA Ops:
  6.5 4.1 %copy-start = (bf16[256,192]{0,1:T(8,128)(2,1)S(1)}, bf16[256,192]{0,1:T(8,128)(2,1)}, u32[]{:S(2)}) copy-start(bf16[256,192]{0,1:T(8,128)(2,1)} %param.6) | copy-start | bytes 294916
  6.5 114.8 %all-gather.2.cloned.1.call-start = ((), (), s32[]{:S(2)}) async-start(), calls=%async_computation.3 | async-start | bytes 8355840 | tf_op jit(solution)/shard_map/all_gather | solution.py:82
  9.9 0.7 copy-start.4
  11.1 35.2 %copy-start.6 = (bf16[6144,8]{0,1:T(8,128)(2,1)S(1)}, bf16[6144,8]{0,1:T(8,128)(2,1)}, u32[]{:S(2)}) copy-start(bf16[6144,8]{0,1:T(8,128)(2,1)} %param.7) | copy-start | bytes 294916
  41.1 0.8 copy-start.1
  42.0 6.2 %copy-start.2 = (bf16[1,6144,256]{2,1,0:T(8,128)(2,1)S(1)}, bf16[1,6144,256]{2,1,0:T(8,128)(2,1)}, u32[]{:S(2)}) copy-start(bf16[1,6144,256]{2,1,0:T(8,128)(2,1)} %param.9) | copy-start | bytes 9437188
  46.2 185.0 %reduce-scatter.2.cloned.1.call-start = ((), (), s32[]{:S(2)}) async-start(), calls=%async_computation.4 | async-start | bytes 8355840 | tf_op jit(solution)/shard_map/reduce_scatter | solution.py:92
  48.2 3.0 %copy-start.3 = (bf16[1,6144,256]{2,1,0:T(8,128)(2,1)S(1)}, bf16[1,6144,256]{2,1,0:T(8,128)(2,1)}, u32[]{:S(2)}) copy-start(bf16[1,6144,256]{2,1,0:T(8,128)(2,1)} %param.10) | copy-start | bytes 9437188
  141.7 120.4 %copy-start.5 = (bf16[256,640]{1,0:T(8,128)(2,1)S(1)}, bf16[256,640]{1,0:T(8,128)(2,1)}, u32[]{:S(2)}) copy-start(bf16[256,640]{1,0:T(8,128)(2,1)} %copy-done.4) | copy-start | bytes 983044
Sparse Core Ops, SparseCore 0:
  46.3 74.9 all-gather.1
  141.9 89.3 reduce-scatter.1

commit v5 on v4

--- a/solution.py
+++ b/solution.py
@@ -72,8 +72,9 @@
         return jnp.swapaxes(w, axis, axis + 1).reshape(shape)
 
     ff_dev = w_gate.shape[2]
+    router_pad = jnp.pad(router_weight, ((0, 0), (0, 128 - n_experts)))
     fused_w = jnp.concatenate(
-        [plane_major(w_gate[0], 0), plane_major(w_up[0], 0), plane_major(router_weight, 0)], axis=1
+        [plane_major(w_gate[0], 0), plane_major(w_up[0], 0), plane_major(router_pad, 0)], axis=1
     )
     down_t = jnp.swapaxes(plane_major(w_down[0], 1), 0, 1)
     contract_first = (((0,), (0,)), ((), ()))
@@ -83,7 +84,7 @@
     fused = lax.dot_general(full, fused_w, contract_first, preferred_element_type=jnp.float32)
     gate = fused[:, :ff_dev]
     upper = fused[:, ff_dev : 2 * ff_dev]
-    logits = fused[:, 2 * ff_dev :]
+    logits = fused[:, 2 * ff_dev : 2 * ff_dev + n_experts]
     own_logit = jnp.sum(jnp.where(expert_col == my_expert, logits, 0.0), axis=1)
     other_logit = jnp.sum(jnp.where(expert_col == other_here[:, None], logits, 0.0), axis=1)
     weight = jax.nn.sigmoid(own_logit - other_logit).astype(jnp.bfloat16).astype(jnp.float32)

time: 270 us -> 269 us (level)
    unnamed x16 -> x17, local copies, waits for them, and re-layouts: 6.8 us -> 8.34 us
    transpose x3 -> x4, local copies, waits for them, and re-layouts: 5.87 us -> 7.31 us  [plane_major(): return jnp.swapaxes(w, axis, axis + 1).reshape(shape)]
where the time goes in v5:
time: 269 us
  waiting for transfers between devices  149 us (55%)
  blocking collectives  58.9 us (22%)
  local copies, waits for them, and re-layouts  20.8 us (8%)
  between operations  13.6 us (5%)
  matrix products  13.5 us (5%)
  Pallas kernels  8.66 us (3%)
  other arithmetic  3.55 us (1%)
    reduce_scatter x1, waiting for transfers between devices, body(): lax.psum_scatter(partial, (GX, GY), scatter_dimension=0, tiled=True)  89.4 us
    all_gather x1, waiting for transfers between devices, body(): full = lax.all_gather(rows_t, (GX, GY), axis=0, tiled=True)  59.9 us
    all_to_all x1, blocking collectives, body(): got = lax.all_to_all(payload, (EXPERT, ZH), 0, 0, tiled=True)  30 us
    all_to_all x1, blocking collectives, body(): got = lax.all_to_all(back, (EXPERT, ZH), 0, 0, tiled=True)  29 us
    dot_general x1, matrix products, body(): lax.dot_general(full, fused_w, contract_first, preferred_element_type=jnp...  12.1 us
    pallas_call x1, Pallas kernels, down_project(): pl.pallas_call(_down_kernel, grid=(d_rows // block,), in_specs=[pl.BlockS...  8.66 us
    unnamed x17, local copies, waits for them, and re-layouts  8.34 us
    transpose x4, local copies, waits for them, and re-layouts, plane_major(): return jnp.swapaxes(w, axis, axis + 1).reshape(shape)  7.31 us
  transfers between devices with their start and end apart: 2, of which 2 were waited for; matrix products, arithmetic and copies ran while one was open for 5% of the time, Pallas kernels for 0%

profile of v5, /device:TPU:1, one launch (start us, length us, event | category | flops | bytes accessed | tf_op | source)
XLA Modules:
  0.0 268.7 jit_solution(4091486268204256839)
XLA Ops:
  6.5 0.8 rev.4
  7.3 0.8 copy.53
  8.8 0.7 multiply_add_fusion
  9.9 0.7 copy-done.4
  11.2 30.0 %all_to_all.10 = bf16[16,200,80]{1,2,0:T(8,128)(2,1)S(1)} all-to-all(bf16[16,200,80]{1,2,0:T(8,128)(2,1)S(1)} %bitcast.54), channel_id=1, replica_groups=mesh['expert'=8,'zh'=2,'x'=4,'y'=4] {'expert','zh'}, dimensions={0} | all-to-all | bytes 1024000 | tf_op jit(solution)/shard_map/all_to_all | solution.py:64
  41.1 0.8 copy-done.1
  42.6 1.1 reshape.101
  44.0 0.8 copy.62
  45.1 1.3 copy.63
  46.4 0.8 copy-done.2
  47.2 2.0 copy.60
  49.2 1.1 copy-done.3
  50.3 2.1 copy.61
  52.4 3.3 %copy.56 = bf16[1,256,6144]{1,2,0:T(8,128)(2,1)S(1)} copy(bf16[1,256,6144]{2,1,0:T(8,128)(2,1)} %param.11) | data formatting | bytes 6291456 | tf_op args[5]
  55.6 1.9 copy.57
  57.6 1.2 convert_reduce_fusion.1
  58.9 59.9 %all-gather.2.cloned.1.call-done = bf16[6144,640]{0,1:T(8,128)(2,1)} async-done(((bf16[384,640]{0,1:T(8,128)(2,1)}), bf16[6144,640]{0,1:T(8,128)(2,1)}) %all-gather.2.cloned.1.call-update) | async-done | bytes 7864336 | tf_op jit(solution)/shard_map/all_gather | solution.py:83
  118.8 12.1 %fusion = f32[640,640]{0,1:T(8,128)S(1)} fusion(bf16[6144,640]{0,1:T(8,128)(2,1)} %all-gather.2.cloned.1.call-done, bf16[6144,128]{1,0:T(8,128)(2,1)} %bitcast.57, bf16[6144,256]{1,0:T(8,128)(2,1)} %bitcast.53, bf16[6144,256]{1,0:T(8,128)(2,1)} %bitcast.52), kind=kOutput, calls=%fused_computation | convolution fusion | flops 5056757760 | bytes 17367040 | tf_op jit(solution)/shard_map/dot_general | solution.py:84
  131.0 1.0 fusion.11.b_ref
  131.9 8.7 %shard_map.64 = bf16[6144,640]{1,0:T(8,128)(2,1)} custom-call(bf16[6144,256]{1,0:T(8,128)(2,1)} %bitcast.46, bf16[256,640]{1,0:T(8,128)(2,1)} %fusion.11.b_ref), custom_call_target="tpu_custom_call" | custom-call | tf_op jit(solution)/shard_map/pallas_call | solution.py:21
  140.6 89.4 %reduce-scatter.2.cloned.1.call-done = bf16[384,640]{1,0:T(8,128)(2,1)} async-done(((bf16[6144,640]{1,0:T(8,128)(2,1)}), bf16[384,640]{1,0:T(8,128)(2,1)}) %reduce-scatter.2.cloned.1.call-update) | async-done | bytes 491536 | tf_op jit(solution)/shard_map/reduce_scatter | solution.py:93
  230.0 1.3 copy.64
  231.8 29.0 %all_to_all.11 = bf16[16,192,80]{1,2,0:T(8,128)(2,1)S(1)} all-to-all(bf16[16,192,80]{1,2,0:T(8,128)(2,1)S(1)} %bitcast.56), channel_id=1, replica_groups=mesh['expert'=8,'zh'=2,'x'=4,'y'=4] {'expert','zh'}, dimensions={0} | all-to-all | bytes 983040 | tf_op jit(solution)/shard_map/all_to_all | solution.py:97
  260.9 1.0 convolution_convert_fusion.1
  (37 shorter events, 3.5 us)
Async XLA Ops:
  6.5 4.1 %copy-start = (bf16[256,192]{0,1:T(8,128)(2,1)S(1)}, bf16[256,192]{0,1:T(8,128)(2,1)}, u32[]{:S(2)}) copy-start(bf16[256,192]{0,1:T(8,128)(2,1)} %param.6) | copy-start | bytes 294916
  6.5 112.3 %all-gather.2.cloned.1.call-start = ((), (), s32[]{:S(2)}) async-start(), calls=%async_computation.3 | async-start | bytes 8355840 | tf_op jit(solution)/shard_map/all_gather | solution.py:83
  9.9 0.7 copy-start.4
  11.1 32.9 %copy-start.6 = (bf16[6144,8]{0,1:T(8,128)(2,1)S(1)}, bf16[6144,8]{0,1:T(8,128)(2,1)}, u32[]{:S(2)}) copy-start(bf16[6144,8]{0,1:T(8,128)(2,1)} %param.7) | copy-start | bytes 294916
  41.1 0.8 copy-start.1
  43.7 186.3 %reduce-scatter.2.cloned.1.call-start = ((), (), s32[]{:S(2)}) async-start(), calls=%async_computation.4 | async-start | bytes 8355840 | tf_op jit(solution)/shard_map/reduce_scatter | solution.py:93
  44.8 2.5 copy-start.2
  47.2 3.0 %copy-start.3 = (bf16[1,6144,256]{2,1,0:T(8,128)(2,1)S(1)}, bf16[1,6144,256]{2,1,0:T(8,128)(2,1)}, u32[]{:S(2)}) copy-start(bf16[1,6144,256]{2,1,0:T(8,128)(2,1)} %param.10) | copy-start | bytes 9437188
  140.6 120.3 %copy-start.5 = (bf16[256,640]{1,0:T(8,128)(2,1)S(1)}, bf16[256,640]{1,0:T(8,128)(2,1)}, u32[]{:S(2)}) copy-start(bf16[256,640]{1,0:T(8,128)(2,1)} %copy-done.4) | copy-start | bytes 983044
Sparse Core Ops, SparseCore 0:
  43.8 74.8 all-gather.1
  140.7 89.2 reduce-scatter.1

commit v6 on v5

--- a/solution.py
+++ b/solution.py
@@ -52,19 +52,21 @@
     other_id = jnp.flip(expert_ids, axis=1).astype(jnp.float32)
     other_of_slot = jnp.sum(placed * other_id[:, :, None], axis=(0, 1))
 
+    my_hi = lax.axis_index(ZH)
+    swap = [(0, 1), (1, 0)]
+    partner = lax.ppermute(tokens, ZH, swap)
+    first_half = jnp.where(my_hi == 0, tokens, partner)
+    second_half = jnp.where(my_hi == 0, partner, tokens)
+    tokens_hi = jnp.concatenate([first_half, second_half], axis=1)
+
     bucket_t = lax.dot_general(
-        tokens, dispatch, (((0,), (0,)), ((), ())), preferred_element_type=jnp.float32
+        tokens_hi, dispatch, (((0,), (0,)), ((), ())), preferred_element_type=jnp.float32
     ).astype(jnp.bfloat16)
     meta = jnp.broadcast_to(other_of_slot.astype(jnp.bfloat16)[None, :], (8, slots_all))
     payload = jnp.concatenate([bucket_t, meta], axis=0)
-    rows_in = payload.shape[0]
-    payload = jnp.swapaxes(payload.reshape(rows_in, n_experts, capacity), 0, 1)
-    payload = jnp.broadcast_to(payload[:, None], (n_experts, n_hi, rows_in, capacity))
-    payload = payload.reshape(n_experts * n_hi, rows_in, capacity)
-    got = lax.all_to_all(payload, (EXPERT, ZH), 0, 0, tiled=True)
-    got = got.reshape(n_experts, n_hi, rows_in, capacity)
-    other_here = got[:, 0, part_width, :].reshape(slots_all).astype(jnp.int32)
-    rows_t = jnp.transpose(got[:, :, :part_width, :], (1, 2, 0, 3)).reshape(n_hi * part_width, slots_all)
+    got = lax.all_to_all(payload, EXPERT, split_axis=1, concat_axis=1, tiled=True)
+    rows_t = got[: n_hi * part_width]
+    other_here = got[n_hi * part_width].astype(jnp.int32)
 
     def plane_major(w, axis):
         shape = w.shape
@@ -92,12 +94,12 @@
     partial = down_project(down_t, hidden.T)
     summed = lax.psum_scatter(partial, (GX, GY), scatter_dimension=0, tiled=True)
 
-    back = summed.reshape(n_hi, part_width, n_experts, capacity)
-    back = jnp.transpose(back, (2, 0, 1, 3)).reshape(n_experts * n_hi, part_width, capacity)
-    got = lax.all_to_all(back, (EXPERT, ZH), 0, 0, tiled=True)
-    got = got.reshape(n_experts, n_hi, part_width, capacity).astype(jnp.float32)
-    returned = jnp.sum(got, axis=1).astype(jnp.bfloat16)
-    returned = jnp.swapaxes(returned, 0, 1).reshape(part_width, slots_all)
+    lower_half = summed[:part_width]
+    upper_half = summed[part_width:]
+    mine = jnp.where(my_hi == 0, lower_half, upper_half)
+    theirs = lax.ppermute(jnp.where(my_hi == 0, upper_half, lower_half), ZH, swap)
+    total = (mine.astype(jnp.float32) + theirs.astype(jnp.float32)).astype(jnp.bfloat16)
+    returned = lax.all_to_all(total, EXPERT, split_axis=1, concat_axis=1, tiled=True)
 
     combine = dispatch
     mixed = lax.dot_general(combine, returned, (((1,), (1,)), ((), ())), preferred_element_type=jnp.float32)

time: 269 us -> 277 us (1.030)
  blocking collectives: 58.9 us -> 44.8 us
  starting transfers between devices: 0.22 us -> 13.3 us
  waiting for transfers between devices: 149 us -> 159 us
  local copies, waits for them, and re-layouts: 20.8 us -> 17.6 us
  other arithmetic: 3.55 us -> 6.59 us
    all_to_all x2, blocking collectives: 58.9 us -> 44.8 us  [the longest x1 22.9 us: body(): lax.all_to_all(payload, EXPERT, split_axis=1, concat_axis=1, tiled=True)]
    ppermute x0 -> x2, starting transfers between devices: none -> 13.3 us  [the longest x1 7.73 us: body(): partner = lax.ppermute(tokens, ZH, swap)]
    all_gather x1, waiting for transfers between devices: 59.9 us -> 64.7 us  [body(): full = lax.all_gather(rows_t, (GX, GY), axis=0, tiled=True)]
    ppermute x0 -> x2, waiting for transfers between devices: none -> 4.22 us  [the longest x1 4.22 us: body(): lax.ppermute(jnp.where(my_hi == 0, upper_half, lower_half), ZH, swap)]
    unnamed x17 -> x11, local copies, waits for them, and re-layouts: 8.34 us -> 7.5 us
  transfers between devices with their start and end apart: 2 -> 4, of which waited for: 2 -> 3; matrix products, arithmetic and copies ran while one was open for 5% -> 6% of each run, Pallas kernels for 0% -> 0%
where the time goes in v6:
time: 277 us
  waiting for transfers between devices  159 us (57%)
  blocking collectives  44.8 us (16%)
  local copies, waits for them, and re-layouts  17.6 us (6%)
  matrix products  13.6 us (5%)
  between operations  13.6 us (5%)
  starting transfers between devices  13.3 us (5%)
  Pallas kernels  8.66 us (3%)
  other arithmetic  6.59 us (2%)
    reduce_scatter x1, waiting for transfers between devices, body(): lax.psum_scatter(partial, (GX, GY), scatter_dimension=0, tiled=True)  89.6 us
    all_gather x1, waiting for transfers between devices, body(): full = lax.all_gather(rows_t, (GX, GY), axis=0, tiled=True)  64.7 us
    all_to_all x1, blocking collectives, body(): lax.all_to_all(payload, EXPERT, split_axis=1, concat_axis=1, tiled=True)  22.9 us
    all_to_all x1, blocking collectives, body(): lax.all_to_all(total, EXPERT, split_axis=1, concat_axis=1, tiled=True)  21.9 us
    dot_general x1, matrix products, body(): lax.dot_general(full, fused_w, contract_first, preferred_element_type=jnp...  12.1 us
    pallas_call x1, Pallas kernels, down_project(): pl.pallas_call(_down_kernel, grid=(d_rows // block,), in_specs=[pl.BlockS...  8.66 us
    ppermute x1, starting transfers between devices, body(): partner = lax.ppermute(tokens, ZH, swap)  7.73 us
    unnamed x11, local copies, waits for them, and re-layouts  7.5 us
  transfers between devices with their start and end apart: 4, of which 3 were waited for; matrix products, arithmetic and copies ran while one was open for 6% of the time, Pallas kernels for 0%

profile of v6, /device:TPU:1, one launch (start us, length us, event | category | flops | bytes accessed | tf_op | source)
XLA Modules:
  0.0 276.7 jit_solution(15720734113248242569)
XLA Ops:
  6.5 7.7 %collective-permute-start = (bf16[256,192]{0,1:T(8,128)(2,1)}, bf16[256,192]{0,1:T(8,128)(2,1)S(1)}, u32[]{:S(2)}, u32[]{:S(2)}) collective-permute-start(bf16[256,192]{0,1:T(8,128)(2,1)} %param.6), channel_id=1, source_target_pairs={{0,16},{16,0},{1,17},{17,1},{2,18},{18,2},{3,19},{19,3},{4,20},{20... | collective-permute-start | bytes 294920 | tf_op jit(solution)/shard_map/ppermute | solution.py:57
  15.0 0.8 copy.46
  17.6 0.9 broadcast_select_fusion.2
  19.2 22.9 %all_to_all.21 = bf16[392,8,80]{0,2,1:T(8,128)(2,1)S(1)} all-to-all(bf16[392,8,80]{0,2,1:T(8,128)(2,1)S(1)} %bitcast.35), channel_id=1, replica_groups=mesh['expert'=8,'zh'=2,'x'=4,'y'=4] {'expert'}, dimensions={1} | all-to-all | bytes 1003520 | tf_op jit(solution)/shard_map/all_to_all | solution.py:67
  42.1 0.8 copy-done.2
  42.9 0.8 slice.33
  45.0 1.3 copy.55
  47.2 2.0 copy.52
  49.1 1.1 copy-done.1
  50.2 2.1 copy.53
  52.3 3.2 %copy.49 = bf16[1,256,6144]{1,2,0:T(8,128)(2,1)S(1)} copy(bf16[1,256,6144]{2,1,0:T(8,128)(2,1)} %param.11) | data formatting | bytes 6291456 | tf_op args[5]
  55.4 1.9 copy.50
  57.4 1.1 convert_reduce_fusion.1
  58.6 64.7 %all-gather.2.cloned.1.call-done = bf16[6144,640]{0,1:T(8,128)(2,1)} async-done(((bf16[384,640]{0,1:T(8,128)(2,1)}), bf16[6144,640]{0,1:T(8,128)(2,1)}) %all-gather.2.cloned.1.call-update) | async-done | bytes 7864336 | tf_op jit(solution)/shard_map/all_gather | solution.py:85
  123.3 12.1 %fusion = f32[640,640]{0,1:T(8,128)S(1)} fusion(bf16[6144,640]{0,1:T(8,128)(2,1)} %all-gather.2.cloned.1.call-done, bf16[6144,128]{1,0:T(8,128)(2,1)} %bitcast.37, bf16[6144,256]{1,0:T(8,128)(2,1)} %bitcast.34, bf16[6144,256]{1,0:T(8,128)(2,1)} %bitcast.33), kind=kOutput, calls=%fused_computation | convolution fusion | flops 5056757760 | bytes 17367040 | tf_op jit(solution)/shard_map/dot_general | solution.py:86
  135.5 1.0 fusion.10.b_ref
  136.5 8.7 %shard_map.64 = bf16[6144,640]{1,0:T(8,128)(2,1)} custom-call(bf16[6144,256]{1,0:T(8,128)(2,1)} %bitcast.29, bf16[256,640]{1,0:T(8,128)(2,1)} %fusion.10.b_ref), custom_call_target="tpu_custom_call" | custom-call | tf_op jit(solution)/shard_map/pallas_call | solution.py:21
  145.1 89.6 %reduce-scatter.2.cloned.1.call-done = bf16[384,640]{1,0:T(8,128)(2,1)} async-done(((bf16[6144,640]{1,0:T(8,128)(2,1)}), bf16[384,640]{1,0:T(8,128)(2,1)}) %reduce-scatter.2.cloned.1.call-update) | async-done | bytes 491536 | tf_op jit(solution)/shard_map/reduce_scatter | solution.py:95
  234.7 1.1 broadcast_select_fusion
  235.8 5.6 %collective-permute-start.1 = (bf16[192,640]{1,0:T(8,128)(2,1)S(1)}, bf16[192,640]{1,0:T(8,128)(2,1)S(1)}, u32[]{:S(2)}, u32[]{:S(2)}) collective-permute-start(bf16[192,640]{1,0:T(8,128)(2,1)S(1)} %broadcast_select_fusion), channel_id=1, source_target_pairs={{0,16},{16,0},{1,17},{17,1},{2,18},{18,2},{3,19},{19,3},{4,20},{20... | collective-permute-start | bytes 737288 | tf_op jit(solution)/shard_map/ppermute | solution.py:100
  241.4 4.2 %collective-permute-done.1 = bf16[192,640]{1,0:T(8,128)(2,1)S(1)} collective-permute-done((bf16[192,640]{1,0:T(8,128)(2,1)S(1)}, bf16[192,640]{1,0:T(8,128)(2,1)S(1)}, u32[]{:S(2)}, u32[]{:S(2)}) %collective-permute-start.1) | collective-permute-done | bytes 245792 | tf_op jit(solution)/shard_map/ppermute | solution.py:100
  245.6 1.2 add_convert_fusion
  246.9 21.9 %all_to_all.22 = bf16[192,8,80]{0,2,1:T(8,128)(2,1)S(1)} all-to-all(bf16[192,8,80]{0,2,1:T(8,128)(2,1)S(1)} %bitcast.39), channel_id=1, replica_groups=mesh['expert'=8,'zh'=2,'x'=4,'y'=4] {'expert'}, dimensions={1} | all-to-all | bytes 491520 | tf_op jit(solution)/shard_map/all_to_all | solution.py:102
  268.9 1.0 convolution_convert_fusion.1
  (32 shorter events, 5.5 us)
Async XLA Ops:
  6.5 116.8 %all-gather.2.cloned.1.call-start = ((), (), s32[]{:S(2)}) async-start(), calls=%async_computation.3 | async-start | bytes 8355840 | tf_op jit(solution)/shard_map/all_gather | solution.py:85
  6.5 11.1 %collective-permute-start = (bf16[256,192]{0,1:T(8,128)(2,1)}, bf16[256,192]{0,1:T(8,128)(2,1)S(1)}, u32[]{:S(2)}, u32[]{:S(2)}) collective-permute-start(bf16[256,192]{0,1:T(8,128)(2,1)} %param.6), channel_id=1, source_target_pairs={{0,16},{16,0},{1,17},{17,1},{2,18},{18,2},{3,19},{19,3},{4,20},{20... | collective-permute-start | bytes 294920 | tf_op jit(solution)/shard_map/ppermute | solution.py:57
  17.6 26.3 %copy-start.3 = (bf16[6144,8]{0,1:T(8,128)(2,1)S(1)}, bf16[6144,8]{0,1:T(8,128)(2,1)}, u32[]{:S(2)}) copy-start(bf16[6144,8]{0,1:T(8,128)(2,1)} %param.7) | copy-start | bytes 294916
  42.1 0.8 copy-start.2
  43.8 190.9 %reduce-scatter.2.cloned.1.call-start = ((), (), s32[]{:S(2)}) async-start(), calls=%async_computation.4 | async-start | bytes 8355840 | tf_op jit(solution)/shard_map/reduce_scatter | solution.py:95
  44.7 2.5 copy-start
  47.1 3.0 %copy-start.1 = (bf16[1,6144,256]{2,1,0:T(8,128)(2,1)S(1)}, bf16[1,6144,256]{2,1,0:T(8,128)(2,1)}, u32[]{:S(2)}) copy-start(bf16[1,6144,256]{2,1,0:T(8,128)(2,1)} %param.10) | copy-start | bytes 9437188
  235.8 9.8 %collective-permute-start.1 = (bf16[192,640]{1,0:T(8,128)(2,1)S(1)}, bf16[192,640]{1,0:T(8,128)(2,1)S(1)}, u32[]{:S(2)}, u32[]{:S(2)}) collective-permute-start(bf16[192,640]{1,0:T(8,128)(2,1)S(1)} %broadcast_select_fusion), channel_id=1, source_target_pairs={{0,16},{16,0},{1,17},{17,1},{2,18},{18,2},{3,19},{19,3},{4,20},{20... | collective-permute-start | bytes 737288 | tf_op jit(solution)/shard_map/ppermute | solution.py:100
Sparse Core Ops, SparseCore 0:
  43.9 79.3 all-gather.1
  145.3 89.3 reduce-scatter.1

commit v7 on v5

--- a/solution.py
+++ b/solution.py
@@ -17,7 +17,7 @@
 def down_project(down_t, hidden_t):
     d_rows, ff = down_t.shape
     rows = hidden_t.shape[1]
-    block = 768
+    block = 1536
     return pl.pallas_call(
         _down_kernel,
         grid=(d_rows // block,),

time: 269 us -> 267 us (level)
  no operation moved by 1% of the time
where the time goes in v7:
time: 267 us
  waiting for transfers between devices  149 us (56%)
  blocking collectives  58.9 us (22%)
  local copies, waits for them, and re-layouts  20.8 us (8%)
  between operations  13.6 us (5%)
  matrix products  13.5 us (5%)
  Pallas kernels  6.86 us (3%)
  other arithmetic  3.55 us (1%)
    reduce_scatter x1, waiting for transfers between devices, body(): lax.psum_scatter(partial, (GX, GY), scatter_dimension=0, tiled=True)  89.3 us
    all_gather x1, waiting for transfers between devices, body(): full = lax.all_gather(rows_t, (GX, GY), axis=0, tiled=True)  59.9 us
    all_to_all x1, blocking collectives, body(): got = lax.all_to_all(payload, (EXPERT, ZH), 0, 0, tiled=True)  30 us
    all_to_all x1, blocking collectives, body(): got = lax.all_to_all(back, (EXPERT, ZH), 0, 0, tiled=True)  28.9 us
    dot_general x1, matrix products, body(): lax.dot_general(full, fused_w, contract_first, preferred_element_type=jnp...  12.1 us
    unnamed x17, local copies, waits for them, and re-layouts  8.34 us
    transpose x4, local copies, waits for them, and re-layouts, plane_major(): return jnp.swapaxes(w, axis, axis + 1).reshape(shape)  7.31 us
    pallas_call x1, Pallas kernels, down_project(): pl.pallas_call(_down_kernel, grid=(d_rows // block,), in_specs=[pl.BlockS...  6.86 us
  transfers between devices with their start and end apart: 2, of which 2 were waited for; matrix products, arithmetic and copies ran while one was open for 5% of the time, Pallas kernels for 0%

profile of v7, /device:TPU:1, one launch (start us, length us, event | category | flops | bytes accessed | tf_op | source)
XLA Modules:
  0.0 266.7 jit_solution(5843848580687596700)
XLA Ops:
  6.5 0.8 rev.4
  7.3 0.8 copy.53
  8.8 0.7 multiply_add_fusion
  9.9 0.7 copy-done.4
  11.2 30.0 %all_to_all.10 = bf16[16,200,80]{1,2,0:T(8,128)(2,1)S(1)} all-to-all(bf16[16,200,80]{1,2,0:T(8,128)(2,1)S(1)} %bitcast.54), channel_id=1, replica_groups=mesh['expert'=8,'zh'=2,'x'=4,'y'=4] {'expert','zh'}, dimensions={0} | all-to-all | bytes 1024000 | tf_op jit(solution)/shard_map/all_to_all | solution.py:64
  41.1 0.8 copy-done.1
  42.6 1.1 reshape.101
  44.0 0.8 copy.62
  45.1 1.3 copy.63
  46.4 0.8 copy-done.2
  47.2 2.0 copy.60
  49.2 1.1 copy-done.3
  50.3 2.1 copy.61
  52.4 3.3 %copy.56 = bf16[1,256,6144]{1,2,0:T(8,128)(2,1)S(1)} copy(bf16[1,256,6144]{2,1,0:T(8,128)(2,1)} %param.11) | data formatting | bytes 6291456 | tf_op args[5]
  55.6 1.9 copy.57
  57.6 1.2 convert_reduce_fusion.1
  58.9 59.9 %all-gather.2.cloned.1.call-done = bf16[6144,640]{0,1:T(8,128)(2,1)} async-done(((bf16[384,640]{0,1:T(8,128)(2,1)}), bf16[6144,640]{0,1:T(8,128)(2,1)}) %all-gather.2.cloned.1.call-update) | async-done | bytes 7864336 | tf_op jit(solution)/shard_map/all_gather | solution.py:83
  118.8 12.1 %fusion = f32[640,640]{0,1:T(8,128)S(1)} fusion(bf16[6144,640]{0,1:T(8,128)(2,1)} %all-gather.2.cloned.1.call-done, bf16[6144,128]{1,0:T(8,128)(2,1)} %bitcast.57, bf16[6144,256]{1,0:T(8,128)(2,1)} %bitcast.53, bf16[6144,256]{1,0:T(8,128)(2,1)} %bitcast.52), kind=kOutput, calls=%fused_computation | convolution fusion | flops 5056757760 | bytes 17367040 | tf_op jit(solution)/shard_map/dot_general | solution.py:84
  131.0 1.0 fusion.11.b_ref
  131.9 6.9 %shard_map.64 = bf16[6144,640]{1,0:T(8,128)(2,1)} custom-call(bf16[6144,256]{1,0:T(8,128)(2,1)} %bitcast.46, bf16[256,640]{1,0:T(8,128)(2,1)} %fusion.11.b_ref), custom_call_target="tpu_custom_call" | custom-call | tf_op jit(solution)/shard_map/pallas_call | solution.py:21
  138.8 89.3 %reduce-scatter.2.cloned.1.call-done = bf16[384,640]{1,0:T(8,128)(2,1)} async-done(((bf16[6144,640]{1,0:T(8,128)(2,1)}), bf16[384,640]{1,0:T(8,128)(2,1)}) %reduce-scatter.2.cloned.1.call-update) | async-done | bytes 491536 | tf_op jit(solution)/shard_map/reduce_scatter | solution.py:93
  228.1 1.3 copy.64
  229.9 28.9 %all_to_all.11 = bf16[16,192,80]{1,2,0:T(8,128)(2,1)S(1)} all-to-all(bf16[16,192,80]{1,2,0:T(8,128)(2,1)S(1)} %bitcast.56), channel_id=1, replica_groups=mesh['expert'=8,'zh'=2,'x'=4,'y'=4] {'expert','zh'}, dimensions={0} | all-to-all | bytes 983040 | tf_op jit(solution)/shard_map/all_to_all | solution.py:97
  258.9 1.0 convolution_convert_fusion.1
  (37 shorter events, 3.5 us)
Async XLA Ops:
  6.5 4.1 %copy-start = (bf16[256,192]{0,1:T(8,128)(2,1)S(1)}, bf16[256,192]{0,1:T(8,128)(2,1)}, u32[]{:S(2)}) copy-start(bf16[256,192]{0,1:T(8,128)(2,1)} %param.6) | copy-start | bytes 294916
  6.5 112.3 %all-gather.2.cloned.1.call-start = ((), (), s32[]{:S(2)}) async-start(), calls=%async_computation.3 | async-start | bytes 8355840 | tf_op jit(solution)/shard_map/all_gather | solution.py:83
  9.9 0.7 copy-start.4
  11.1 32.9 %copy-start.6 = (bf16[6144,8]{0,1:T(8,128)(2,1)S(1)}, bf16[6144,8]{0,1:T(8,128)(2,1)}, u32[]{:S(2)}) copy-start(bf16[6144,8]{0,1:T(8,128)(2,1)} %param.7) | copy-start | bytes 294916
  41.1 0.8 copy-start.1
  43.7 184.4 %reduce-scatter.2.cloned.1.call-start = ((), (), s32[]{:S(2)}) async-start(), calls=%async_computation.4 | async-start | bytes 8355840 | tf_op jit(solution)/shard_map/reduce_scatter | solution.py:93
  44.8 2.5 copy-start.2
  47.2 3.0 %copy-start.3 = (bf16[1,6144,256]{2,1,0:T(8,128)(2,1)S(1)}, bf16[1,6144,256]{2,1,0:T(8,128)(2,1)}, u32[]{:S(2)}) copy-start(bf16[1,6144,256]{2,1,0:T(8,128)(2,1)} %param.10) | copy-start | bytes 9437188
  138.8 120.1 %copy-start.5 = (bf16[256,640]{1,0:T(8,128)(2,1)S(1)}, bf16[256,640]{1,0:T(8,128)(2,1)}, u32[]{:S(2)}) copy-start(bf16[256,640]{1,0:T(8,128)(2,1)} %copy-done.4) | copy-start | bytes 983044
Sparse Core Ops, SparseCore 0:
  43.8 74.8 all-gather.1
  138.9 89.1 reduce-scatter.1

commit v8 on v7

--- a/solution.py
+++ b/solution.py
@@ -17,7 +17,7 @@
 def down_project(down_t, hidden_t):
     d_rows, ff = down_t.shape
     rows = hidden_t.shape[1]
-    block = 1536
+    block = 3072
     return pl.pallas_call(
         _down_kernel,
         grid=(d_rows // block,),

time: 267 us -> 267 us (level)
  no operation moved by 1% of the time
where the time goes in v8:
time: 267 us; the launch traced here: 266 us
  waiting for transfers between devices  149 us (56%)
  blocking collectives  58.9 us (22%)
  local copies, waits for them, and re-layouts  20.8 us (8%)
  between operations  13.6 us (5%)
  matrix products  13.5 us (5%)
  Pallas kernels  6.14 us (2%)
  other arithmetic  3.55 us (1%)
    reduce_scatter x1, waiting for transfers between devices, body(): lax.psum_scatter(partial, (GX, GY), scatter_dimension=0, tiled=True)  89.4 us
    all_gather x1, waiting for transfers between devices, body(): full = lax.all_gather(rows_t, (GX, GY), axis=0, tiled=True)  59.9 us
    all_to_all x1, blocking collectives, body(): got = lax.all_to_all(payload, (EXPERT, ZH), 0, 0, tiled=True)  30 us
    all_to_all x1, blocking collectives, body(): got = lax.all_to_all(back, (EXPERT, ZH), 0, 0, tiled=True)  28.9 us
    dot_general x1, matrix products, body(): lax.dot_general(full, fused_w, contract_first, preferred_element_type=jnp...  12.1 us
    unnamed x17, local copies, waits for them, and re-layouts  8.34 us
    transpose x4, local copies, waits for them, and re-layouts, plane_major(): return jnp.swapaxes(w, axis, axis + 1).reshape(shape)  7.31 us
    pallas_call x1, Pallas kernels, down_project(): pl.pallas_call(_down_kernel, grid=(d_rows // block,), in_specs=[pl.BlockS...  6.14 us
  transfers between devices with their start and end apart: 2, of which 2 were waited for; matrix products, arithmetic and copies ran while one was open for 5% of the time, Pallas kernels for 0%

profile of v8, /device:TPU:1, one launch (start us, length us, event | category | flops | bytes accessed | tf_op | source)
XLA Modules:
  0.0 266.2 jit_solution(9501074981159809559)
XLA Ops:
  6.5 0.8 rev.4
  7.3 0.8 copy.53
  8.8 0.7 multiply_add_fusion
  9.9 0.7 copy-done.4
  11.2 30.0 %all_to_all.10 = bf16[16,200,80]{1,2,0:T(8,128)(2,1)S(1)} all-to-all(bf16[16,200,80]{1,2,0:T(8,128)(2,1)S(1)} %bitcast.54), channel_id=1, replica_groups=mesh['expert'=8,'zh'=2,'x'=4,'y'=4] {'expert','zh'}, dimensions={0} | all-to-all | bytes 1024000 | tf_op jit(solution)/shard_map/all_to_all | solution.py:64
  41.1 0.8 copy-done.1
  42.6 1.1 reshape.101
  44.0 0.8 copy.62
  45.1 1.3 copy.63
  46.4 0.8 copy-done.2
  47.2 2.0 copy.60
  49.2 1.1 copy-done.3
  50.3 2.1 copy.61
  52.4 3.3 %copy.56 = bf16[1,256,6144]{1,2,0:T(8,128)(2,1)S(1)} copy(bf16[1,256,6144]{2,1,0:T(8,128)(2,1)} %param.11) | data formatting | bytes 6291456 | tf_op args[5]
  55.6 1.9 copy.57
  57.6 1.2 convert_reduce_fusion.1
  58.9 59.9 %all-gather.2.cloned.1.call-done = bf16[6144,640]{0,1:T(8,128)(2,1)} async-done(((bf16[384,640]{0,1:T(8,128)(2,1)}), bf16[6144,640]{0,1:T(8,128)(2,1)}) %all-gather.2.cloned.1.call-update) | async-done | bytes 7864336 | tf_op jit(solution)/shard_map/all_gather | solution.py:83
  118.8 12.1 %fusion = f32[640,640]{0,1:T(8,128)S(1)} fusion(bf16[6144,640]{0,1:T(8,128)(2,1)} %all-gather.2.cloned.1.call-done, bf16[6144,128]{1,0:T(8,128)(2,1)} %bitcast.57, bf16[6144,256]{1,0:T(8,128)(2,1)} %bitcast.53, bf16[6144,256]{1,0:T(8,128)(2,1)} %bitcast.52), kind=kOutput, calls=%fused_computation | convolution fusion | flops 5056757760 | bytes 17367040 | tf_op jit(solution)/shard_map/dot_general | solution.py:84
  131.0 1.0 fusion.11.b_ref
  131.9 6.1 %shard_map.64 = bf16[6144,640]{1,0:T(8,128)(2,1)} custom-call(bf16[6144,256]{1,0:T(8,128)(2,1)} %bitcast.46, bf16[256,640]{1,0:T(8,128)(2,1)} %fusion.11.b_ref), custom_call_target="tpu_custom_call" | custom-call | tf_op jit(solution)/shard_map/pallas_call | solution.py:21
  138.1 89.4 %reduce-scatter.2.cloned.1.call-done = bf16[384,640]{1,0:T(8,128)(2,1)} async-done(((bf16[6144,640]{1,0:T(8,128)(2,1)}), bf16[384,640]{1,0:T(8,128)(2,1)}) %reduce-scatter.2.cloned.1.call-update) | async-done | bytes 491536 | tf_op jit(solution)/shard_map/reduce_scatter | solution.py:93
  227.6 1.3 copy.64
  229.3 28.9 %all_to_all.11 = bf16[16,192,80]{1,2,0:T(8,128)(2,1)S(1)} all-to-all(bf16[16,192,80]{1,2,0:T(8,128)(2,1)S(1)} %bitcast.56), channel_id=1, replica_groups=mesh['expert'=8,'zh'=2,'x'=4,'y'=4] {'expert','zh'}, dimensions={0} | all-to-all | bytes 983040 | tf_op jit(solution)/shard_map/all_to_all | solution.py:97
  258.4 1.0 convolution_convert_fusion.1
  (37 shorter events, 3.5 us)
Async XLA Ops:
  6.5 4.1 %copy-start = (bf16[256,192]{0,1:T(8,128)(2,1)S(1)}, bf16[256,192]{0,1:T(8,128)(2,1)}, u32[]{:S(2)}) copy-start(bf16[256,192]{0,1:T(8,128)(2,1)} %param.6) | copy-start | bytes 294916
  6.5 112.3 %all-gather.2.cloned.1.call-start = ((), (), s32[]{:S(2)}) async-start(), calls=%async_computation.3 | async-start | bytes 8355840 | tf_op jit(solution)/shard_map/all_gather | solution.py:83
  9.9 0.7 copy-start.4
  11.1 32.9 %copy-start.6 = (bf16[6144,8]{0,1:T(8,128)(2,1)S(1)}, bf16[6144,8]{0,1:T(8,128)(2,1)}, u32[]{:S(2)}) copy-start(bf16[6144,8]{0,1:T(8,128)(2,1)} %param.7) | copy-start | bytes 294916
  41.1 0.8 copy-start.1
  43.7 183.8 %reduce-scatter.2.cloned.1.call-start = ((), (), s32[]{:S(2)}) async-start(), calls=%async_computation.4 | async-start | bytes 8355840 | tf_op jit(solution)/shard_map/reduce_scatter | solution.py:93
  44.8 2.5 copy-start.2
  47.2 3.0 %copy-start.3 = (bf16[1,6144,256]{2,1,0:T(8,128)(2,1)S(1)}, bf16[1,6144,256]{2,1,0:T(8,128)(2,1)}, u32[]{:S(2)}) copy-start(bf16[1,6144,256]{2,1,0:T(8,128)(2,1)} %param.10) | copy-start | bytes 9437188
  138.1 120.3 %copy-start.5 = (bf16[256,640]{1,0:T(8,128)(2,1)S(1)}, bf16[256,640]{1,0:T(8,128)(2,1)}, u32[]{:S(2)}) copy-start(bf16[256,640]{1,0:T(8,128)(2,1)} %copy-done.4) | copy-start | bytes 983044
Sparse Core Ops, SparseCore 0:
  43.8 74.8 all-gather.1
  138.2 89.2 reduce-scatter.1

commit v9 on v8

--- a/solution.py
+++ b/solution.py
@@ -58,23 +58,26 @@
     meta = jnp.broadcast_to(other_of_slot.astype(jnp.bfloat16)[None, :], (8, slots_all))
     payload = jnp.concatenate([bucket_t, meta], axis=0)
     rows_in = payload.shape[0]
-    payload = jnp.swapaxes(payload.reshape(rows_in, n_experts, capacity), 0, 1)
-    payload = jnp.broadcast_to(payload[:, None], (n_experts, n_hi, rows_in, capacity))
-    payload = payload.reshape(n_experts * n_hi, rows_in, capacity)
-    got = lax.all_to_all(payload, (EXPERT, ZH), 0, 0, tiled=True)
-    got = got.reshape(n_experts, n_hi, rows_in, capacity)
-    other_here = got[:, 0, part_width, :].reshape(slots_all).astype(jnp.int32)
-    rows_t = jnp.transpose(got[:, :, :part_width, :], (1, 2, 0, 3)).reshape(n_hi * part_width, slots_all)
+    payload = jnp.broadcast_to(payload[:, None], (rows_in, n_hi, slots_all)).reshape(rows_in, n_hi * slots_all)
+    got = lax.all_to_all(payload, (ZH, EXPERT), 1, 1, tiled=True)
+    got = got.reshape(rows_in, n_hi, slots_all)
+    other_here = got[part_width, 0].astype(jnp.int32)
+    rows_t = got[:part_width].reshape(part_width * n_hi, slots_all)
 
     def plane_major(w, axis):
         shape = w.shape
         w = w.reshape(shape[:axis] + (n_hi, n_plane, part_width) + shape[axis + 1 :])
         return jnp.swapaxes(w, axis, axis + 1).reshape(shape)
 
+    def feature_minor(w):
+        tail = w.shape[1:]
+        w = w.reshape((n_hi, n_plane, part_width) + tail)
+        return jnp.moveaxis(w, 0, 2).reshape((d_model,) + tail)
+
     ff_dev = w_gate.shape[2]
     router_pad = jnp.pad(router_weight, ((0, 0), (0, 128 - n_experts)))
     fused_w = jnp.concatenate(
-        [plane_major(w_gate[0], 0), plane_major(w_up[0], 0), plane_major(router_pad, 0)], axis=1
+        [feature_minor(w_gate[0]), feature_minor(w_up[0]), feature_minor(router_pad)], axis=1
     )
     down_t = jnp.swapaxes(plane_major(w_down[0], 1), 0, 1)
     contract_first = (((0,), (0,)), ((), ()))

time: 267 us -> 260 us (0.974)
  waiting for transfers between devices: 149 us -> 131 us
  local copies, waits for them, and re-layouts: 20.8 us -> 32.8 us
    all_gather x1, waiting for transfers between devices: 59.9 us -> 42.5 us  [body(): full = lax.all_gather(rows_t, (GX, GY), axis=0, tiled=True)]
    another operation x0 -> x2, local copies, waits for them, and re-layouts: none -> 10.5 us  [feature_minor(): w = w.reshape((n_hi, n_plane, part_width) + tail)]
    reshape x1 -> x3, local copies, waits for them, and re-layouts: 1.14 us -> 7.84 us  [the longest x2 6.44 us: feature_minor(): return jnp.moveaxis(w, 0, 2).reshape((d_model,) + tail)]
    transpose x4 -> x1, local copies, waits for them, and re-layouts: 7.31 us -> 1.95 us  [plane_major(): return jnp.swapaxes(w, axis, axis + 1).reshape(shape)]
    unnamed x17 -> x13, local copies, waits for them, and re-layouts: 8.34 us -> 5.74 us
  transfers between devices with their start and end apart: 2 -> 2, of which waited for: 2 -> 2; matrix products, arithmetic and copies ran while one was open for 5% -> 11% of each run, Pallas kernels for 0% -> 0%
where the time goes in v9:
time: 260 us
  waiting for transfers between devices  131 us (50%)
  blocking collectives  59 us (23%)
  local copies, waits for them, and re-layouts  32.8 us (13%)
  between operations  13.6 us (5%)
  matrix products  13.5 us (5%)
  Pallas kernels  6.14 us (2%)
  other arithmetic  3.49 us (1%)
    reduce_scatter x1, waiting for transfers between devices, body(): lax.psum_scatter(partial, (GX, GY), scatter_dimension=0, tiled=True)  88.7 us
    all_gather x1, waiting for transfers between devices, body(): full = lax.all_gather(rows_t, (GX, GY), axis=0, tiled=True)  42.5 us
    all_to_all x1, blocking collectives, body(): got = lax.all_to_all(payload, (ZH, EXPERT), 1, 1, tiled=True)  30 us
    all_to_all x1, blocking collectives, body(): got = lax.all_to_all(back, (EXPERT, ZH), 0, 0, tiled=True)  29 us
    dot_general x1, matrix products, body(): lax.dot_general(full, fused_w, contract_first, preferred_element_type=jnp...  12.1 us
    another operation x2, local copies, waits for them, and re-layouts, feature_minor(): w = w.reshape((n_hi, n_plane, part_width) + tail)  10.5 us
    reshape x2, local copies, waits for them, and re-layouts, feature_minor(): return jnp.moveaxis(w, 0, 2).reshape((d_model,) + tail)  6.44 us
    pallas_call x1, Pallas kernels, down_project(): pl.pallas_call(_down_kernel, grid=(d_rows // block,), in_specs=[pl.BlockS...  6.14 us
  transfers between devices with their start and end apart: 2, of which 2 were waited for; matrix products, arithmetic and copies ran while one was open for 11% of the time, Pallas kernels for 0%

profile of v9, /device:TPU:1, one launch (start us, length us, event | category | flops | bytes accessed | tf_op | source)
XLA Modules:
  0.0 260.0 jit_solution(5720586806588739120)
XLA Ops:
  6.5 0.8 copy.54
  8.0 0.7 multiply_add_fusion
  8.7 0.7 rev.4
  9.9 0.7 copy-done.2
  11.2 30.0 %all_to_all.14 = bf16[200,16,80]{0,2,1:T(8,128)(2,1)S(1)} all-to-all(bf16[200,16,80]{0,2,1:T(8,128)(2,1)S(1)} %bitcast.48), channel_id=1, replica_groups=mesh['expert'=8,'zh'=2,'x'=4,'y'=4] {'zh','expert'}, dimensions={1} | all-to-all | bytes 1024000 | tf_op jit(solution)/shard_map/all_to_all | solution.py:62
  41.1 0.7 copy.60
  41.8 1.4 reshape.101
  43.5 5.1 %copy.70 = bf16[2,16,192,256]{3,0,2,1:T(2,128)(2,1)S(1)} copy(bf16[2,16,192,256]{3,2,1,0:T(8,128)(2,1)} %bitcast.46) | data formatting | bytes 6291456 | tf_op jit(solution)/shard_map/reshape;squeeze | solution.py:74
  48.6 3.2 %reshape.102 = bf16[6144,256]{1,0:T(8,128)(2,1)} reshape(bf16[16,192,2,256]{3,2,1,0:T(2,128)(2,1)S(1)} %bitcast.39) | data formatting | bytes 6291456 | tf_op jit(solution)/shard_map/reshape | solution.py:75
  51.8 5.3 %copy.69 = bf16[2,16,192,256]{3,0,2,1:T(2,128)(2,1)S(1)} copy(bf16[2,16,192,256]{3,2,1,0:T(8,128)(2,1)} %bitcast.47) | data formatting | bytes 6291456 | tf_op jit(solution)/shard_map/reshape;squeeze | solution.py:74
  57.2 3.2 %reshape.103 = bf16[6144,256]{1,0:T(8,128)(2,1)} reshape(bf16[16,192,2,256]{3,2,1,0:T(2,128)(2,1)S(1)} %bitcast.40) | data formatting | bytes 6291456 | tf_op jit(solution)/shard_map/reshape | solution.py:75
  60.4 0.8 copy.63
  61.5 2.8 %copy.64 = bf16[16,192,2,128]{3,2,1,0:T(2,128)(2,1)} copy(bf16[16,192,2,128]{3,1,0,2:T(8,128)(2,1)S(1)} %bitcast.43) | data formatting | bytes 3145728 | tf_op jit(solution)/shard_map/transpose | solution.py:75
  64.3 3.4 %copy.57 = bf16[1,256,6144]{1,2,0:T(8,128)(2,1)S(1)} copy(bf16[1,256,6144]{2,1,0:T(8,128)(2,1)} %param.11) | data formatting | bytes 6291456 | tf_op args[5]
  67.7 1.9 copy.58
  69.7 1.2 convert_reduce_fusion.1
  70.8 42.5 %all-gather.2.cloned.1.call-done = bf16[6144,640]{1,0:T(8,128)(2,1)} async-done(((bf16[384,640]{1,0:T(8,128)(2,1)}), bf16[6144,640]{1,0:T(8,128)(2,1)}) %all-gather.2.cloned.1.call-update) | async-done | bytes 7864336 | tf_op jit(solution)/shard_map/all_gather | solution.py:86
  113.3 12.1 %fusion = f32[640,640]{0,1:T(8,128)S(1)} fusion(bf16[6144,640]{1,0:T(8,128)(2,1)} %all-gather.2.cloned.1.call-done, bf16[6144,128]{1,0:T(8,128)(2,1)} %bitcast.51, bf16[6144,256]{1,0:T(8,128)(2,1)} %reshape.103, bf16[6144,256]{1,0:T(8,128)(2,1)} %reshape.102), kind=kOutput, calls=%fused_computation | convolution fusion | flops 5056757760 | bytes 17367040 | tf_op jit(solution)/shard_map/dot_general | solution.py:87
  125.5 1.0 fusion.11.b_ref
  126.4 6.1 %shard_map.64 = bf16[6144,640]{1,0:T(8,128)(2,1)} custom-call(bf16[6144,256]{1,0:T(8,128)(2,1)} %bitcast.42, bf16[256,640]{1,0:T(8,128)(2,1)} %fusion.11.b_ref), custom_call_target="tpu_custom_call" | custom-call | tf_op jit(solution)/shard_map/pallas_call | solution.py:21
  132.6 88.7 %reduce-scatter.2.cloned.1.call-done = bf16[384,640]{1,0:T(8,128)(2,1)} async-done(((bf16[6144,640]{1,0:T(8,128)(2,1)}), bf16[384,640]{1,0:T(8,128)(2,1)}) %reduce-scatter.2.cloned.1.call-update) | async-done | bytes 491536 | tf_op jit(solution)/shard_map/reduce_scatter | solution.py:96
  221.3 1.3 copy.65
  223.1 29.0 %all_to_all.15 = bf16[16,192,80]{1,2,0:T(8,128)(2,1)S(1)} all-to-all(bf16[16,192,80]{1,2,0:T(8,128)(2,1)S(1)} %bitcast.50), channel_id=1, replica_groups=mesh['expert'=8,'zh'=2,'x'=4,'y'=4] {'expert','zh'}, dimensions={0} | all-to-all | bytes 983040 | tf_op jit(solution)/shard_map/all_to_all | solution.py:100
  252.2 1.0 convolution_convert_fusion.1
  (33 shorter events, 2.8 us)
Async XLA Ops:
  6.5 4.1 %copy-start = (bf16[256,192]{0,1:T(8,128)(2,1)S(1)}, bf16[256,192]{0,1:T(8,128)(2,1)}, u32[]{:S(2)}) copy-start(bf16[256,192]{0,1:T(8,128)(2,1)} %param.6) | copy-start | bytes 294916
  6.5 106.8 %all-gather.2.cloned.1.call-start = ((), (), s32[]{:S(2)}) async-start(), calls=%async_computation.3 | async-start | bytes 8355840 | tf_op jit(solution)/shard_map/all_gather | solution.py:86
  9.9 0.7 copy-start.2
  41.1 2.3 copy-start.1
  43.2 178.1 %reduce-scatter.2.cloned.1.call-start = ((), (), s32[]{:S(2)}) async-start(), calls=%async_computation.4 | async-start | bytes 8355840 | tf_op jit(solution)/shard_map/reduce_scatter | solution.py:96
  57.2 3.2 %copy-start.4 = (bf16[6144,8]{0,1:T(8,128)(2,1)S(1)}, bf16[6144,8]{0,1:T(8,128)(2,1)}, u32[]{:S(2)}) copy-start(bf16[6144,8]{0,1:T(8,128)(2,1)} %param.7) | copy-start | bytes 294916
  132.6 119.6 %copy-start.3 = (bf16[256,640]{1,0:T(8,128)(2,1)S(1)}, bf16[256,640]{1,0:T(8,128)(2,1)}, u32[]{:S(2)}) copy-start(bf16[256,640]{1,0:T(8,128)(2,1)} %copy-done.2) | copy-start | bytes 983044
Sparse Core Ops, SparseCore 0:
  43.3 69.9 all-gather.1
  132.7 88.5 reduce-scatter.1

commit v10 on v9

--- a/solution.py
+++ b/solution.py
@@ -79,7 +79,7 @@
     fused_w = jnp.concatenate(
         [feature_minor(w_gate[0]), feature_minor(w_up[0]), feature_minor(router_pad)], axis=1
     )
-    down_t = jnp.swapaxes(plane_major(w_down[0], 1), 0, 1)
+    down_t = feature_minor(jnp.swapaxes(w_down[0], 0, 1))
     contract_first = (((0,), (0,)), ((), ()))
     expert_col = jnp.arange(n_experts, dtype=jnp.int32)[None, :]
 
@@ -95,12 +95,10 @@
     partial = down_project(down_t, hidden.T)
     summed = lax.psum_scatter(partial, (GX, GY), scatter_dimension=0, tiled=True)
 
-    back = summed.reshape(n_hi, part_width, n_experts, capacity)
-    back = jnp.transpose(back, (2, 0, 1, 3)).reshape(n_experts * n_hi, part_width, capacity)
-    got = lax.all_to_all(back, (EXPERT, ZH), 0, 0, tiled=True)
-    got = got.reshape(n_experts, n_hi, part_width, capacity).astype(jnp.float32)
+    back = summed.reshape(part_width, n_hi * slots_all)
+    got = lax.all_to_all(back, (ZH, EXPERT), 1, 1, tiled=True)
+    got = got.reshape(part_width, n_hi, slots_all).astype(jnp.float32)
     returned = jnp.sum(got, axis=1).astype(jnp.bfloat16)
-    returned = jnp.swapaxes(returned, 0, 1).reshape(part_width, slots_all)
 
     combine = dispatch
     mixed = lax.dot_general(combine, returned, (((1,), (1,)), ((), ())), preferred_element_type=jnp.float32)

time: 260 us -> 261 us (level)
  local copies, waits for them, and re-layouts: 32.8 us -> 39.9 us
  waiting for transfers between devices: 131 us -> 125 us
    all_gather x1, waiting for transfers between devices: 42.5 us -> 36.5 us  [body(): full = lax.all_gather(rows_t, (GX, GY), axis=0, tiled=True)]
    transpose x1 -> x2, local copies, waits for them, and re-layouts: 2.81 us -> 7.94 us  [feature_minor(): return jnp.moveaxis(w, 0, 2).reshape((d_model,) + tail)]
    reshape x2 -> x3, local copies, waits for them, and re-layouts: 6.44 us -> 9.95 us  [feature_minor(): return jnp.moveaxis(w, 0, 2).reshape((d_model,) + tail)]
    all_to_all x0 -> x2, local copies, waits for them, and re-layouts: none -> 2.61 us  [body(): got = lax.all_to_all(back, (ZH, EXPERT), 1, 1, tiled=True)]
    unnamed x13 -> x15, local copies, waits for them, and re-layouts: 5.74 us -> 5.25 us
  transfers between devices with their start and end apart: 2 -> 2, of which waited for: 2 -> 2; matrix products, arithmetic and copies ran while one was open for 11% -> 13% of each run, Pallas kernels for 0% -> 0%
where the time goes in v10:
time: 261 us
  waiting for transfers between devices  125 us (48%)
  blocking collectives  59 us (23%)
  local copies, waits for them, and re-layouts  39.9 us (15%)
  between operations  13.6 us (5%)
  matrix products  13.5 us (5%)
  Pallas kernels  6.14 us (2%)
  other arithmetic  3.49 us (1%)
    reduce_scatter x1, waiting for transfers between devices, body(): lax.psum_scatter(partial, (GX, GY), scatter_dimension=0, tiled=True)  88.7 us
    all_gather x1, waiting for transfers between devices, body(): full = lax.all_gather(rows_t, (GX, GY), axis=0, tiled=True)  36.5 us
    all_to_all x1, blocking collectives, body(): got = lax.all_to_all(payload, (ZH, EXPERT), 1, 1, tiled=True)  30 us
    all_to_all x1, blocking collectives, body(): got = lax.all_to_all(back, (ZH, EXPERT), 1, 1, tiled=True)  29 us
    dot_general x1, matrix products, body(): lax.dot_general(full, fused_w, contract_first, preferred_element_type=jnp...  12.1 us
    another operation x2, local copies, waits for them, and re-layouts, feature_minor(): w = w.reshape((n_hi, n_plane, part_width) + tail)  10.5 us
    reshape x3, local copies, waits for them, and re-layouts, feature_minor(): return jnp.moveaxis(w, 0, 2).reshape((d_model,) + tail)  9.95 us
    transpose x2, local copies, waits for them, and re-layouts, feature_minor(): return jnp.moveaxis(w, 0, 2).reshape((d_model,) + tail)  7.94 us
  transfers between devices with their start and end apart: 2, of which 2 were waited for; matrix products, arithmetic and copies ran while one was open for 13% of the time, Pallas kernels for 0%

profile of v10, /device:TPU:1, one launch (start us, length us, event | category | flops | bytes accessed | tf_op | source)
XLA Modules:
  0.0 260.9 jit_solution(6740867528030570251)
XLA Ops:
  6.5 0.8 copy.64
  8.0 0.7 multiply_add_fusion
  8.7 0.7 rev.4
  9.9 0.7 copy-done.3
  11.2 30.0 %all_to_all.18 = bf16[200,16,80]{0,2,1:T(8,128)(2,1)S(1)} all-to-all(bf16[200,16,80]{0,2,1:T(8,128)(2,1)S(1)} %bitcast.42), channel_id=1, replica_groups=mesh['expert'=8,'zh'=2,'x'=4,'y'=4] {'zh','expert'}, dimensions={1} | all-to-all | bytes 1024000 | tf_op jit(solution)/shard_map/all_to_all | solution.py:62
  41.8 1.4 reshape.101
  43.3 5.1 %copy.79 = bf16[2,16,192,256]{3,0,2,1:T(2,128)(2,1)S(1)} copy(bf16[2,16,192,256]{3,2,1,0:T(8,128)(2,1)} %bitcast.40) | data formatting | bytes 6291456 | tf_op jit(solution)/shard_map/reshape;squeeze | solution.py:74
  48.4 3.4 %reshape.102 = bf16[6144,256]{1,0:T(8,128)(2,1)} reshape(bf16[16,192,2,256]{3,2,1,0:T(2,128)(2,1)S(1)} %bitcast.34) | data formatting | bytes 6291456 | tf_op jit(solution)/shard_map/reshape | solution.py:75
  51.8 5.3 %copy.78 = bf16[2,16,192,256]{3,0,2,1:T(2,128)(2,1)S(1)} copy(bf16[2,16,192,256]{3,2,1,0:T(8,128)(2,1)} %bitcast.41) | data formatting | bytes 6291456 | tf_op jit(solution)/shard_map/reshape;squeeze | solution.py:74
  57.2 3.2 %reshape.103 = bf16[6144,256]{1,0:T(8,128)(2,1)} reshape(bf16[16,192,2,256]{3,2,1,0:T(2,128)(2,1)S(1)} %bitcast.35) | data formatting | bytes 6291456 | tf_op jit(solution)/shard_map/reshape | solution.py:75
  60.4 0.8 copy.73
  61.5 2.8 %copy.74 = bf16[16,192,2,128]{3,2,1,0:T(2,128)(2,1)} copy(bf16[16,192,2,128]{3,1,0,2:T(8,128)(2,1)S(1)} %bitcast.37) | data formatting | bytes 3145728 | tf_op jit(solution)/shard_map/transpose | solution.py:75
  64.3 2.9 %copy.67 = bf16[1,256,6144]{1,2,0:T(8,128)(2,1)} copy(bf16[1,256,6144]{2,1,0:T(8,128)(2,1)S(1)} %copy-done.2) | data formatting | bytes 6291456 | tf_op args[5]
  67.2 5.1 %copy.68 = bf16[16,192,2,256]{3,2,1,0:T(2,128)(2,1)S(1)} copy(bf16[16,192,2,256]{3,1,0,2:T(8,128)(2,1)} %bitcast.36) | data formatting | bytes 6291456 | tf_op jit(solution)/shard_map/transpose | solution.py:75
  72.4 3.3 %reshape.100.a_ref = bf16[6144,256]{1,0:T(8,128)(2,1)} reshape(bf16[16,192,2,256]{3,2,1,0:T(2,128)(2,1)S(1)} %copy.68) | data formatting | bytes 6291456 | tf_op jit(solution)/shard_map/reshape | solution.py:75
  75.7 1.2 convert_reduce_fusion.1
  76.9 36.5 %all-gather.2.cloned.1.call-done = bf16[6144,640]{1,0:T(8,128)(2,1)} async-done(((bf16[384,640]{1,0:T(8,128)(2,1)}), bf16[6144,640]{1,0:T(8,128)(2,1)}) %all-gather.2.cloned.1.call-update) | async-done | bytes 7864336 | tf_op jit(solution)/shard_map/all_gather | solution.py:86
  113.3 12.1 %fusion = f32[640,640]{0,1:T(8,128)S(1)} fusion(bf16[6144,640]{1,0:T(8,128)(2,1)} %all-gather.2.cloned.1.call-done, bf16[6144,128]{1,0:T(8,128)(2,1)} %bitcast.44, bf16[6144,256]{1,0:T(8,128)(2,1)} %reshape.103, bf16[6144,256]{1,0:T(8,128)(2,1)} %reshape.102), kind=kOutput, calls=%fused_computation | convolution fusion | flops 5056757760 | bytes 17367040 | tf_op jit(solution)/shard_map/dot_general | solution.py:87
  125.5 1.0 fusion.11.b_ref
  126.4 6.1 %shard_map.64 = bf16[6144,640]{1,0:T(8,128)(2,1)} custom-call(bf16[6144,256]{1,0:T(8,128)(2,1)} %reshape.100.a_ref, bf16[256,640]{1,0:T(8,128)(2,1)} %fusion.11.b_ref), custom_call_target="tpu_custom_call" | custom-call | tf_op jit(solution)/shard_map/pallas_call | solution.py:21
  132.6 88.7 %reduce-scatter.2.cloned.1.call-done = bf16[384,640]{1,0:T(8,128)(2,1)} async-done(((bf16[6144,640]{1,0:T(8,128)(2,1)}), bf16[384,640]{1,0:T(8,128)(2,1)}) %reduce-scatter.2.cloned.1.call-update) | async-done | bytes 491536 | tf_op jit(solution)/shard_map/reduce_scatter | solution.py:96
  221.3 1.9 all_to_all.14
  224.0 29.0 %all_to_all.19 = bf16[192,16,80]{0,2,1:T(8,128)(2,1)S(1)} all-to-all(bf16[192,16,80]{0,2,1:T(8,128)(2,1)S(1)} %copy.75), channel_id=1, replica_groups=mesh['expert'=8,'zh'=2,'x'=4,'y'=4] {'zh','expert'}, dimensions={1} | all-to-all | bytes 983040 | tf_op jit(solution)/shard_map/all_to_all | solution.py:99
  253.1 1.0 convolution_convert_fusion.1
  (35 shorter events, 3.5 us)
Async XLA Ops:
  6.5 4.1 %copy-start = (bf16[256,192]{0,1:T(8,128)(2,1)S(1)}, bf16[256,192]{0,1:T(8,128)(2,1)}, u32[]{:S(2)}) copy-start(bf16[256,192]{0,1:T(8,128)(2,1)} %param.6) | copy-start | bytes 294916
  6.5 106.8 %all-gather.2.cloned.1.call-start = ((), (), s32[]{:S(2)}) async-start(), calls=%async_computation.3 | async-start | bytes 8355840 | tf_op jit(solution)/shard_map/all_gather | solution.py:86
  9.9 0.7 copy-start.3
  41.1 2.1 copy-start.1
  43.2 178.1 %reduce-scatter.2.cloned.1.call-start = ((), (), s32[]{:S(2)}) async-start(), calls=%async_computation.4 | async-start | bytes 8355840 | tf_op jit(solution)/shard_map/reduce_scatter | solution.py:96
  57.2 3.2 %copy-start.5 = (bf16[6144,8]{0,1:T(8,128)(2,1)S(1)}, bf16[6144,8]{0,1:T(8,128)(2,1)}, u32[]{:S(2)}) copy-start(bf16[6144,8]{0,1:T(8,128)(2,1)} %param.7) | copy-start | bytes 294916
  61.5 2.8 %copy-start.2 = (bf16[1,256,6144]{2,1,0:T(8,128)(2,1)S(1)}, bf16[1,256,6144]{2,1,0:T(8,128)(2,1)}, u32[]{:S(2)}) copy-start(bf16[1,256,6144]{2,1,0:T(8,128)(2,1)} %param.11) | copy-start | bytes 9437188
  132.6 120.5 %copy-start.4 = (bf16[256,640]{1,0:T(8,128)(2,1)S(1)}, bf16[256,640]{1,0:T(8,128)(2,1)}, u32[]{:S(2)}) copy-start(bf16[256,640]{1,0:T(8,128)(2,1)} %copy-done.3) | copy-start | bytes 983044
Sparse Core Ops, SparseCore 0:
  43.3 69.9 all-gather.1
  132.7 88.5 reduce-scatter.1

commit v11 on v9

--- a/solution.py
+++ b/solution.py
@@ -75,9 +75,8 @@
         return jnp.moveaxis(w, 0, 2).reshape((d_model,) + tail)
 
     ff_dev = w_gate.shape[2]
-    router_pad = jnp.pad(router_weight, ((0, 0), (0, 128 - n_experts)))
     fused_w = jnp.concatenate(
-        [feature_minor(w_gate[0]), feature_minor(w_up[0]), feature_minor(router_pad)], axis=1
+        [feature_minor(w_gate[0]), feature_minor(w_up[0]), feature_minor(router_weight)], axis=1
     )
     down_t = jnp.swapaxes(plane_major(w_down[0], 1), 0, 1)
     contract_first = (((0,), (0,)), ((), ()))

time: 260 us -> 259 us (level)
    transpose x1 -> x0, local copies, waits for them, and re-layouts: 2.81 us -> none  [feature_minor(): return jnp.moveaxis(w, 0, 2).reshape((d_model,) + tail)]
    reshape x0 -> x2, local copies, waits for them, and re-layouts: none -> 2.6 us  [feature_minor(): w = w.reshape((n_hi, n_plane, part_width) + tail)]
    unnamed x13 -> x12, local copies, waits for them, and re-layouts: 5.74 us -> 4.74 us
  transfers between devices with their start and end apart: 2 -> 2, of which waited for: 2 -> 2; matrix products, arithmetic and copies ran while one was open for 11% -> 10% of each run, Pallas kernels for 0% -> 0%
where the time goes in v11:
time: 259 us; the launch traced here: 258 us
  waiting for transfers between devices  133 us (51%)
  blocking collectives  58.9 us (23%)
  local copies, waits for them, and re-layouts  31.5 us (12%)
  between operations  13.6 us (5%)
  matrix products  12.2 us (5%)
  Pallas kernels  6.14 us (2%)
  other arithmetic  3.49 us (1%)
    reduce_scatter x1, waiting for transfers between devices, body(): lax.psum_scatter(partial, (GX, GY), scatter_dimension=0, tiled=True)  88.5 us
    all_gather x1, waiting for transfers between devices, body(): full = lax.all_gather(rows_t, (GX, GY), axis=0, tiled=True)  44 us
    all_to_all x1, blocking collectives, body(): got = lax.all_to_all(payload, (ZH, EXPERT), 1, 1, tiled=True)  30 us
    all_to_all x1, blocking collectives, body(): got = lax.all_to_all(back, (EXPERT, ZH), 0, 0, tiled=True)  29 us
    dot_general x1, matrix products, body(): lax.dot_general(full, fused_w, contract_first, preferred_element_type=jnp...  10.7 us
    another operation x2, local copies, waits for them, and re-layouts, feature_minor(): w = w.reshape((n_hi, n_plane, part_width) + tail)  10.5 us
    reshape x2, local copies, waits for them, and re-layouts, feature_minor(): return jnp.moveaxis(w, 0, 2).reshape((d_model,) + tail)  6.63 us
    pallas_call x1, Pallas kernels, down_project(): pl.pallas_call(_down_kernel, grid=(d_rows // block,), in_specs=[pl.BlockS...  6.14 us
  transfers between devices with their start and end apart: 2, of which 2 were waited for; matrix products, arithmetic and copies ran while one was open for 10% of the time, Pallas kernels for 0%

profile of v11, /device:TPU:1, one launch (start us, length us, event | category | flops | bytes accessed | tf_op | source)
XLA Modules:
  0.0 258.4 jit_solution(5228877253373543409)
XLA Ops:
  6.5 0.8 copy.51
  8.0 0.7 multiply_add_fusion
  8.7 0.7 rev.4
  9.5 0.4 convert_reduce_fusion
  9.9 0.7 copy-done.2
  11.2 30.0 %all_to_all.14 = bf16[200,16,80]{0,2,1:T(8,128)(2,1)S(1)} all-to-all(bf16[200,16,80]{0,2,1:T(8,128)(2,1)S(1)} %bitcast.48), channel_id=1, replica_groups=mesh['expert'=8,'zh'=2,'x'=4,'y'=4] {'zh','expert'}, dimensions={1} | all-to-all | bytes 1024000 | tf_op jit(solution)/shard_map/all_to_all | solution.py:62
  41.1 0.7 copy.57
  41.8 1.4 reshape.101
  43.3 5.1 %copy.66 = bf16[2,16,192,256]{3,0,2,1:T(2,128)(2,1)S(1)} copy(bf16[2,16,192,256]{3,2,1,0:T(8,128)(2,1)} %bitcast.46) | data formatting | bytes 6291456 | tf_op jit(solution)/shard_map/reshape;squeeze | solution.py:74
  48.4 3.4 %reshape.102 = bf16[6144,256]{1,0:T(8,128)(2,1)} reshape(bf16[16,192,2,256]{3,2,1,0:T(2,128)(2,1)S(1)} %bitcast.40) | data formatting | bytes 6291456 | tf_op jit(solution)/shard_map/reshape | solution.py:75
  51.8 5.3 %copy.65 = bf16[2,16,192,256]{3,0,2,1:T(2,128)(2,1)S(1)} copy(bf16[2,16,192,256]{3,2,1,0:T(8,128)(2,1)} %bitcast.47) | data formatting | bytes 6291456 | tf_op jit(solution)/shard_map/reshape;squeeze | solution.py:74
  57.2 3.2 %reshape.103 = bf16[6144,256]{1,0:T(8,128)(2,1)} reshape(bf16[16,192,2,256]{3,2,1,0:T(2,128)(2,1)S(1)} %bitcast.41) | data formatting | bytes 6291456 | tf_op jit(solution)/shard_map/reshape | solution.py:75
  60.6 2.4 copy.60
  63.0 3.2 %copy.54 = bf16[1,256,6144]{1,2,0:T(8,128)(2,1)S(1)} copy(bf16[1,256,6144]{2,1,0:T(8,128)(2,1)} %param.11) | data formatting | bytes 6291456 | tf_op args[5]
  66.2 1.9 copy.55
  68.1 1.2 convert_reduce_fusion.1
  69.3 44.0 %all-gather.2.cloned.1.call-done = bf16[6144,640]{1,0:T(8,128)(2,1)} async-done(((bf16[384,640]{1,0:T(8,128)(2,1)}), bf16[6144,640]{1,0:T(8,128)(2,1)}) %all-gather.2.cloned.1.call-update) | async-done | bytes 7864336 | tf_op jit(solution)/shard_map/all_gather | solution.py:85
  113.3 10.7 %fusion = f32[640,520]{0,1:T(8,128)S(1)} fusion(bf16[6144,640]{1,0:T(8,128)(2,1)} %all-gather.2.cloned.1.call-done, bf16[6144,8]{1,0:T(8,128)(2,1)} %bitcast.51, bf16[6144,256]{1,0:T(8,128)(2,1)} %reshape.103, bf16[6144,256]{1,0:T(8,128)(2,1)} %reshape.102), kind=kOutput, calls=%fused_computation | convolution fusion | flops 4108615680 | bytes 15585280 | tf_op jit(solution)/shard_map/dot_general | solution.py:86
  124.2 1.0 fusion.11.b_ref
  125.1 6.1 %shard_map.64 = bf16[6144,640]{1,0:T(8,128)(2,1)} custom-call(bf16[6144,256]{1,0:T(8,128)(2,1)} %bitcast.43, bf16[256,640]{1,0:T(8,128)(2,1)} %fusion.11.b_ref), custom_call_target="tpu_custom_call" | custom-call | tf_op jit(solution)/shard_map/pallas_call | solution.py:21
  131.3 88.5 %reduce-scatter.2.cloned.1.call-done = bf16[384,640]{1,0:T(8,128)(2,1)} async-done(((bf16[6144,640]{1,0:T(8,128)(2,1)}), bf16[384,640]{1,0:T(8,128)(2,1)}) %reduce-scatter.2.cloned.1.call-update) | async-done | bytes 491536 | tf_op jit(solution)/shard_map/reduce_scatter | solution.py:95
  219.8 1.3 copy.61
  221.5 29.0 %all_to_all.15 = bf16[16,192,80]{1,2,0:T(8,128)(2,1)S(1)} all-to-all(bf16[16,192,80]{1,2,0:T(8,128)(2,1)S(1)} %bitcast.50), channel_id=1, replica_groups=mesh['expert'=8,'zh'=2,'x'=4,'y'=4] {'expert','zh'}, dimensions={0} | all-to-all | bytes 983040 | tf_op jit(solution)/shard_map/all_to_all | solution.py:99
  250.6 1.0 convolution_convert_fusion.1
  (32 shorter events, 2.1 us)
Async XLA Ops:
  6.5 4.1 %copy-start = (bf16[256,192]{0,1:T(8,128)(2,1)S(1)}, bf16[256,192]{0,1:T(8,128)(2,1)}, u32[]{:S(2)}) copy-start(bf16[256,192]{0,1:T(8,128)(2,1)} %param.6) | copy-start | bytes 294916
  6.5 106.8 %all-gather.2.cloned.1.call-start = ((), (), s32[]{:S(2)}) async-start(), calls=%async_computation.3 | async-start | bytes 8355840 | tf_op jit(solution)/shard_map/all_gather | solution.py:85
  9.9 0.7 copy-start.2
  41.1 2.1 copy-start.1
  43.2 176.6 %reduce-scatter.2.cloned.1.call-start = ((), (), s32[]{:S(2)}) async-start(), calls=%async_computation.4 | async-start | bytes 8355840 | tf_op jit(solution)/shard_map/reduce_scatter | solution.py:95
  57.2 3.2 %copy-start.4 = (bf16[6144,8]{0,1:T(8,128)(2,1)S(1)}, bf16[6144,8]{0,1:T(8,128)(2,1)}, u32[]{:S(2)}) copy-start(bf16[6144,8]{0,1:T(8,128)(2,1)} %param.7) | copy-start | bytes 294916
  131.3 119.3 %copy-start.3 = (bf16[256,640]{1,0:T(8,128)(2,1)S(1)}, bf16[256,640]{1,0:T(8,128)(2,1)}, u32[]{:S(2)}) copy-start(bf16[256,640]{1,0:T(8,128)(2,1)} %copy-done.2) | copy-start | bytes 983044
Sparse Core Ops, SparseCore 0:
  43.3 69.9 all-gather.1
  131.4 88.3 reduce-scatter.1
